TPU v7x, 256 devices: a whole 4x4x8 slice. The times are simulated.
256 devices in a mesh: dp: 8 (over y_hi, x), seq: 16 (over y_lo, z), segment: 2 (over core).
Axes of the slice: x: 4, y: 4 (y_hi: 2, y_lo: 2; y = y_hi * 2 + y_lo), z: 8, core: 2. Of those that a mesh axis runs over, the one named last changes fastest.
Arguments:
- saved_input: bfloat16 [2, 8, 8192, 256], P('segment', 'dp', 'seq'), may hold values from -6 to 6
- upstream: bfloat16 [8, 8192, 256], P('dp', 'seq'), may hold values from -6 to 6
- clip_lengths: int32 [8, 32], P('dp'), may hold values from 1 to 2048, 8192 in all within a row
- conv_a: bfloat16 [2, 3, 7, 256, 256], P('segment'), may hold values from -0.125 to 0.125
- bias_a: float32 [2, 3, 256], P('segment'), may hold values from -3 to 3
- conv_b: bfloat16 [2, 3, 256, 256], P('segment'), may hold values from -0.375 to 0.375
Outputs:
- section_input_grad: bfloat16 [2, 8, 8192, 256], P('segment', 'dp', 'seq')
- grad_conv_a: float32 [2, 3, 7, 256, 256], P('segment')
- grad_bias_a: float32 [2, 3, 256], P('segment')
- grad_conv_b: float32 [2, 3, 256, 256], P('segment')
Inputs may be any that keep to these rules, and one draw needn't show every extreme that they name: `clip_lengths`: each row's 32 lengths sum to 8192, and the longest is exactly 2048.
All inputs are finite; a program needn't handle non-finite values.
Results may differ from a plain program's by a relative error of at most 0.02.
Values may be sent and summed in bfloat16 or wider, within the bound.
No kernel may reach another device: no remote copies, remote signals or barrier semaphores. Data moves between devices by JAX's collectives and lax.ppermute only.
A program may use at most 128 MiB of HBM per device.

v0:
```python
import jax
import jax.numpy as jnp
from jax import lax
from jax.sharding import PartitionSpec as P

KERNEL = 7
UNITS = 3


def with_halo(cells, sides, width):
    for axis, dim in sides:
        count = lax.axis_size(axis)
        ends = count - 1
        head = lax.slice_in_dim(cells, 0, width, axis=dim)
        tail = lax.slice_in_dim(cells, cells.shape[dim] - width, cells.shape[dim], axis=dim)
        cells = jnp.concatenate(
            [
                lax.ppermute(tail, axis, [(i, (i + 1) % count) for i in range(ends)]),
                cells,
                lax.ppermute(head, axis, [((i + 1) % count, i) for i in range(ends)]),
            ],
            axis=dim,
        )
    return cells


def spread(value, axis, root):
    mine = lax.axis_index(axis) == root
    return lax.psum(jnp.where(mine, value, jnp.zeros_like(value)), axis)


def elu_act(value):
    return jnp.where(value > 0, value, jnp.expm1(jnp.minimum(value, 0.0)))


def elu_slope(value):
    return jnp.where(value > 0, 1.0, jnp.exp(jnp.minimum(value, 0.0)))


def spread_acts(active, reach):
    return with_halo(active, (("seq", 0),), reach)


def spread_grads(gate, reach):
    return with_halo(gate, (("seq", 0),), reach)


def shards(saved_input, upstream, clip_lengths, conv_a, bias_a, conv_b):
    stream = saved_input[0, 0]
    lengths = clip_lengths[0]
    weights_a = conv_a[0]
    biases_a = bias_a[0]
    weights_b = conv_b[0]
    frames = stream.shape[0]
    channels = stream.shape[1]
    inner = weights_a.shape[3]
    half = KERNEL // 2
    furthest = half * 3 ** (UNITS - 1)
    offset = lax.axis_index("seq") * frames
    is_decoder = lax.axis_index("segment") == 1
    clip_ends = jnp.cumsum(lengths)
    places = offset - furthest + jnp.arange(frames + 2 * furthest, dtype=jnp.int32)
    clip_of = jnp.sum((places[:, None] >= clip_ends[None, :]).astype(jnp.int32), axis=1)
    own_clip = clip_of[furthest : furthest + frames]

    def linked(shift_by):
        return (clip_of[furthest + shift_by : furthest + shift_by + frames] == own_clip)[:, None]

    stored = []
    for unit_idx in range(UNITS):
        dilation = 3**unit_idx
        reach = half * dilation
        active = elu_act(stream.astype(jnp.float32)).astype(jnp.bfloat16)
        padded = spread_acts(active, reach)
        tap_rows = jnp.concatenate(
            [
                jnp.where(
                    linked((tap_no - half) * dilation),
                    padded[
                        reach
                        + (tap_no - half) * dilation : reach
                        + (tap_no - half) * dilation
                        + frames
                    ],
                    jnp.zeros((), jnp.bfloat16),
                )
                for tap_no in range(KERNEL)
            ],
            axis=1,
        )
        pre_act = biases_a[unit_idx][None, :] + jnp.dot(
            tap_rows,
            weights_a[unit_idx].reshape(KERNEL * channels, inner),
            preferred_element_type=jnp.float32,
        )
        squashed = elu_act(pre_act).astype(jnp.bfloat16)
        next_stream = (
            stream.astype(jnp.float32)
            + jnp.dot(squashed, weights_b[unit_idx], preferred_element_type=jnp.float32)
        ).astype(jnp.bfloat16)
        stored.append((stream, tap_rows, pre_act, squashed))
        stream = next_stream

    def unit_back(unit_idx, grad_y):
        dilation = 3**unit_idx
        reach = half * dilation
        stream_in, tap_rows, pre_act, squashed = stored[unit_idx]
        grad_b = lax.dot_general(
            grad_y,
            weights_b[unit_idx],
            (((1,), (1,)), ((), ())),
            preferred_element_type=jnp.float32,
        )
        gate = (grad_b * elu_slope(pre_act)).astype(jnp.bfloat16)
        gate_padded = spread_grads(gate, reach)
        back_rows = jnp.concatenate(
            [
                jnp.where(
                    linked(-(tap_no - half) * dilation),
                    gate_padded[
                        reach
                        - (tap_no - half) * dilation : reach
                        - (tap_no - half) * dilation
                        + frames
                    ],
                    jnp.zeros((), jnp.bfloat16),
                )
                for tap_no in range(KERNEL)
            ],
            axis=1,
        )
        turned = jnp.transpose(weights_a[unit_idx], (0, 2, 1)).reshape(KERNEL * inner, channels)
        back = jnp.dot(back_rows, turned, preferred_element_type=jnp.float32)
        grad_next = (
            grad_y.astype(jnp.float32) + back * elu_slope(stream_in.astype(jnp.float32))
        ).astype(jnp.bfloat16)
        return (gate, grad_next)

    first_gates = [None] * UNITS
    first_grads = [None] * (UNITS + 1)
    grad_y = upstream[0]
    first_grads[UNITS] = grad_y
    for unit_idx in reversed(range(UNITS)):
        gate, grad_y = unit_back(unit_idx, grad_y)
        first_gates[unit_idx] = gate
        first_grads[unit_idx] = grad_y
    latent = spread(grad_y, "segment", 1)
    grads_a = [None] * UNITS
    grads_bias = [None] * UNITS
    grads_b = [None] * UNITS
    contract = (((0,), (0,)), ((), ()))
    grad_y = latent
    for unit_idx in reversed(range(UNITS)):
        stream_in, tap_rows, pre_act, squashed = stored[unit_idx]
        gate_two, grad_next = unit_back(unit_idx, grad_y)
        gate = jnp.where(is_decoder, first_gates[unit_idx], gate_two)
        grad_out = jnp.where(is_decoder, first_grads[unit_idx + 1], grad_y)
        unit_b = lax.dot_general(squashed, grad_out, contract, preferred_element_type=jnp.float32)
        unit_bias = jnp.sum(gate.astype(jnp.float32), axis=0)
        unit_a = lax.dot_general(
            tap_rows, gate, contract, preferred_element_type=jnp.float32
        ).reshape(KERNEL, channels, inner)
        grads_a[unit_idx] = unit_a
        grads_bias[unit_idx] = unit_bias
        grads_b[unit_idx] = unit_b
        grad_y = grad_next
    section_grad = jnp.where(is_decoder, first_grads[0], grad_y)
    total_a = jnp.stack(grads_a)
    total_bias = jnp.stack(grads_bias)
    total_b = jnp.stack(grads_b)
    total_a, total_bias, total_b = lax.psum((total_a, total_bias, total_b), ("dp", "seq"))
    return (section_grad[None, None], total_a[None], total_bias[None], total_b[None])


def solution(mesh):
    placed = (
        P("segment", "dp", "seq", None),
        P("dp", "seq", None),
        P("dp", None),
        P("segment", None, None, None, None),
        P("segment", None, None),
        P("segment", None, None, None),
    )
    return jax.shard_map(
        shards,
        mesh=mesh,
        in_specs=placed,
        out_specs=(
            P("segment", "dp", "seq", None),
            P("segment", None, None, None, None),
            P("segment", None, None),
            P("segment", None, None, None),
        ),
        check_vma=False,
    )
```

profile of v0, /device:TPU:32, one launch (start us, length us, event | category | flops | bytes accessed | tf_op | source)
XLA Modules:
  0.0 530.8 jit_solution(7893162154168476364)
XLA Ops:
  8.4 3.7 collective-permute-start.1
  12.1 2.1 collective-permute-start
  15.6 3.7 slice_bitcast_fusion.2
  21.9 3.8 collective-permute-start.2
  25.7 2.0 collective-permute-start.3
  28.3 4.1 collective-permute-done.3
  34.5 3.9 collective-permute-start.4
  38.5 1.9 collective-permute-start.5
  40.9 4.3 collective-permute-done.5
  47.8 1.9 collective-permute-start.6
  49.7 2.2 copy.20
  52.0 4.1 collective-permute-start.7
  61.3 1.9 collective-permute-start.8
  63.3 2.2 copy.21
  65.5 4.1 collective-permute-start.9
  74.6 1.9 collective-permute-start.10
  77.9 4.4 collective-permute-start.11
  85.3 1.5 broadcast_select_fusion.3
  86.9 37.4 %all-reduce.4.cloned.1.call-done = bf16[512,256]{1,0:T(8,128)(2,1)} async-done(((bf16[512,256]{1,0:T(8,128)(2,1)}), bf16[512,256]{1,0:T(8,128)(2,1)}) %all-reduce.4.cloned.1.call-update) | async-done | bytes 262160 | tf_op jit(solution)/shard_map/psum | solution.py:29
  124.3 2.1 convert_reduce_fusion
  126.4 2.3 fusion.203
  128.7 3.5 collective-permute-start.13
  132.2 2.4 collective-permute-start.12
  135.0 2.8 collective-permute-done.12
  141.3 2.4 collective-permute-start.14
  144.1 3.9 collective-permute-start.15
  152.8 2.8 maximum_bitcast_fusion
  157.2 1.9 collective-permute-start.16
  159.1 349.1 %psum.30 = f32[1,3,256]{2,0,1:T(1,128)} all-reduce(f32[1,3,256]{2,0,1:T(1,128)S(1)} %broadcast_in_dim.397), channel_id=1, replica_groups=mesh['dp'=8,'seq'=16,'segment'=2] {'dp','seq'}, use_global_device_ids=true, to_apply=%region_7.8 | all-reduce | flops 768 | bytes 6144 | tf_op jit(solution)/shard_map/psum | solution.py:171
  508.2 2.0 collective-permute-start.17
  510.8 4.8 collective-permute-done.17
  517.4 5.6 %copy.80 = f32[1,3,7,256,256]{4,3,2,1,0:T(8,128)} copy(f32[1,3,7,256,256]{4,3,2,1,0:T(8,128)} %get-tuple-element.60) | data formatting | bytes 11010048
  (275 shorter events, 38.2 us)
Async XLA Ops:
  7.2 117.1 %all-reduce.4.cloned.1.call-start = ((), (), s32[]{:S(2)}) async-start(), calls=%async_computation | async-start | bytes 524288 | tf_op jit(solution)/shard_map/psum | solution.py:29
  8.4 11.6 %collective-permute-start.1 = (bf16[3,256]{1,0:T(4,128)(2,1)S(1)}, bf16[3,256]{1,0:T(4,128)(2,1)S(1)}, u32[]{:S(2)}, u32[]{:S(2)}) collective-permute-start(bf16[3,256]{1,0:T(4,128)(2,1)S(1)} %get-tuple-element.28), channel_id=1, source_target_pairs={{2,0},{4,2},{6,4},{8,6},{10,8},{12,10},{14,12},{16,14},{18,16},{20... | collective-permute-start | bytes 4616 | tf_op jit(solution)/shard_map/ppermute | solution.py:20
  12.1 7.2 %collective-permute-start = (bf16[3,256]{1,0:T(4,128)(2,1)S(1)}, bf16[3,256]{1,0:T(4,128)(2,1)S(1)}, u32[]{:S(2)}, u32[]{:S(2)}) collective-permute-start(bf16[3,256]{1,0:T(4,128)(2,1)S(1)} %get-tuple-element.29), channel_id=1, source_target_pairs={{0,2},{2,4},{4,6},{6,8},{8,10},{10,12},{12,14},{14,16},{16,18},{18... | collective-permute-start | bytes 4616 | tf_op jit(solution)/shard_map/ppermute | solution.py:18
  15.4 25.0 %copy-start.52 = (pred[512]{0:T(512)(128)(4,1)}, pred[512]{0:T(512)(128)(4,1)S(1)}, u32[]{:S(2)}) copy-start(pred[512]{0:T(512)(128)(4,1)S(1)} %get-tuple-element.43) | copy-start | bytes 1540
  15.4 30.0 %copy-start.55 = (pred[512]{0:T(512)(128)(4,1)}, pred[512]{0:T(512)(128)(4,1)S(1)}, u32[]{:S(2)}) copy-start(pred[512]{0:T(512)(128)(4,1)S(1)} %get-tuple-element.39) | copy-start | bytes 1540
  15.5 17.0 %copy-start.38 = (pred[512]{0:T(512)(128)(4,1)}, pred[512]{0:T(512)(128)(4,1)S(1)}, u32[]{:S(2)}) copy-start(pred[512]{0:T(512)(128)(4,1)S(1)} %get-tuple-element.33) | copy-start | bytes 1540
  15.5 25.0 %copy-start.41 = (pred[512]{0:T(512)(128)(4,1)}, pred[512]{0:T(512)(128)(4,1)S(1)}, u32[]{:S(2)}) copy-start(pred[512]{0:T(512)(128)(4,1)S(1)} %get-tuple-element.31) | copy-start | bytes 1540
  15.5 25.2 %copy-start.24 = (pred[512]{0:T(512)(128)(4,1)}, pred[512]{0:T(512)(128)(4,1)S(1)}, u32[]{:S(2)}) copy-start(pred[512]{0:T(512)(128)(4,1)S(1)} %get-tuple-element.35) | copy-start | bytes 1540
  15.6 29.7 %copy-start.27 = (pred[512]{0:T(512)(128)(4,1)}, pred[512]{0:T(512)(128)(4,1)S(1)}, u32[]{:S(2)}) copy-start(pred[512]{0:T(512)(128)(4,1)S(1)} %get-tuple-element.32) | copy-start | bytes 1540
  15.6 30.0 %copy-start.44 = (pred[512]{0:T(512)(128)(4,1)}, pred[512]{0:T(512)(128)(4,1)S(1)}, u32[]{:S(2)}) copy-start(pred[512]{0:T(512)(128)(4,1)S(1)} %get-tuple-element.30) | copy-start | bytes 1540
  21.9 5.9 %collective-permute-start.2 = (bf16[9,256]{1,0:T(8,128)(2,1)S(1)}, bf16[9,256]{1,0:T(8,128)(2,1)S(1)}, u32[]{:S(2)}, u32[]{:S(2)}) collective-permute-start(bf16[9,256]{1,0:T(8,128)(2,1)S(1)} %get-tuple-element.27), channel_id=1, source_target_pairs={{0,2},{2,4},{4,6},{6,8},{8,10},{10,12},{12,14},{14,16},{16,18},{18... | collective-permute-start | bytes 13832 | tf_op jit(solution)/shard_map/ppermute | solution.py:18
  25.7 6.7 %collective-permute-start.3 = (bf16[9,256]{1,0:T(8,128)(2,1)S(1)}, bf16[9,256]{1,0:T(8,128)(2,1)S(1)}, u32[]{:S(2)}, u32[]{:S(2)}) collective-permute-start(bf16[9,256]{1,0:T(8,128)(2,1)S(1)} %get-tuple-element.26), channel_id=1, source_target_pairs={{2,0},{4,2},{6,4},{8,6},{10,8},{12,10},{14,12},{16,14},{18,16},{20... | collective-permute-start | bytes 13832 | tf_op jit(solution)/shard_map/ppermute | solution.py:20
  34.5 24.4 %copy-start.18 = (f32[512,256]{1,0:T(8,128)}, f32[512,256]{1,0:T(8,128)S(1)}, u32[]{:S(2)}) copy-start(f32[512,256]{1,0:T(8,128)S(1)} %get-tuple-element.50) | copy-start | bytes 1572868
  34.5 5.9 %collective-permute-start.4 = (bf16[27,256]{1,0:T(8,128)(2,1)S(1)}, bf16[27,256]{1,0:T(8,128)(2,1)S(1)}, u32[]{:S(2)}, u32[]{:S(2)}) collective-permute-start(bf16[27,256]{1,0:T(8,128)(2,1)S(1)} %get-tuple-element.25), channel_id=1, source_target_pairs={{0,2},{2,4},{4,6},{6,8},{8,10},{10,12},{12,14},{14,16},{16,18},{18... | collective-permute-start | bytes 41480 | tf_op jit(solution)/shard_map/ppermute | solution.py:18
  38.5 6.7 %collective-permute-start.5 = (bf16[27,256]{1,0:T(8,128)(2,1)S(1)}, bf16[27,256]{1,0:T(8,128)(2,1)S(1)}, u32[]{:S(2)}, u32[]{:S(2)}) collective-permute-start(bf16[27,256]{1,0:T(8,128)(2,1)S(1)} %get-tuple-element.24), channel_id=1, source_target_pairs={{2,0},{4,2},{6,4},{8,6},{10,8},{12,10},{14,12},{16,14},{18,16},{20... | collective-permute-start | bytes 41480 | tf_op jit(solution)/shard_map/ppermute | solution.py:20
  47.8 8.2 %collective-permute-start.6 = (bf16[27,256]{1,0:T(8,128)(2,1)}, bf16[27,256]{1,0:T(8,128)(2,1)S(1)}, u32[]{:S(2)}, u32[]{:S(2)}) collective-permute-start(bf16[27,256]{1,0:T(8,128)(2,1)} %get-tuple-element.23), channel_id=1, source_target_pairs={{2,0},{4,2},{6,4},{8,6},{10,8},{12,10},{14,12},{16,14},{18,16},{20... | collective-permute-start | bytes 41480 | tf_op jit(solution)/shard_map/ppermute | solution.py:20
  52.0 6.5 %collective-permute-start.7 = (bf16[27,256]{1,0:T(8,128)(2,1)}, bf16[27,256]{1,0:T(8,128)(2,1)S(1)}, u32[]{:S(2)}, u32[]{:S(2)}) collective-permute-start(bf16[27,256]{1,0:T(8,128)(2,1)} %get-tuple-element.22), channel_id=1, source_target_pairs={{0,2},{2,4},{4,6},{6,8},{8,10},{10,12},{12,14},{14,16},{16,18},{18... | collective-permute-start | bytes 41480 | tf_op jit(solution)/shard_map/ppermute | solution.py:18
  61.3 8.3 %collective-permute-start.8 = (bf16[9,256]{1,0:T(8,128)(2,1)S(1)}, bf16[9,256]{1,0:T(8,128)(2,1)S(1)}, u32[]{:S(2)}, u32[]{:S(2)}) collective-permute-start(bf16[9,256]{1,0:T(8,128)(2,1)S(1)} %get-tuple-element.21), channel_id=1, source_target_pairs={{2,0},{4,2},{6,4},{8,6},{10,8},{12,10},{14,12},{16,14},{18,16},{20... | collective-permute-start | bytes 13832 | tf_op jit(solution)/shard_map/ppermute | solution.py:20
  65.5 5.7 %collective-permute-start.9 = (bf16[9,256]{1,0:T(8,128)(2,1)S(1)}, bf16[9,256]{1,0:T(8,128)(2,1)S(1)}, u32[]{:S(2)}, u32[]{:S(2)}) collective-permute-start(bf16[9,256]{1,0:T(8,128)(2,1)S(1)} %get-tuple-element.20), channel_id=1, source_target_pairs={{0,2},{2,4},{4,6},{6,8},{8,10},{10,12},{12,14},{14,16},{16,18},{18... | collective-permute-start | bytes 13832 | tf_op jit(solution)/shard_map/ppermute | solution.py:18
  74.6 7.7 %collective-permute-start.10 = (bf16[3,256]{1,0:T(4,128)(2,1)}, bf16[3,256]{1,0:T(4,128)(2,1)}, u32[]{:S(2)}, u32[]{:S(2)}) collective-permute-start(bf16[3,256]{1,0:T(4,128)(2,1)} %get-tuple-element.19), channel_id=1, source_target_pairs={{2,0},{4,2},{6,4},{8,6},{10,8},{12,10},{14,12},{16,14},{18,16},{20... | collective-permute-start | bytes 4616 | tf_op jit(solution)/shard_map/ppermute | solution.py:20
  77.9 6.9 %collective-permute-start.11 = (bf16[3,256]{1,0:T(4,128)(2,1)}, bf16[3,256]{1,0:T(4,128)(2,1)S(1)}, u32[]{:S(2)}, u32[]{:S(2)}) collective-permute-start(bf16[3,256]{1,0:T(4,128)(2,1)} %get-tuple-element.18), channel_id=1, source_target_pairs={{0,2},{2,4},{4,6},{6,8},{8,10},{10,12},{12,14},{14,16},{16,18},{18... | collective-permute-start | bytes 4616 | tf_op jit(solution)/shard_map/ppermute | solution.py:18
  86.8 430.6 %all-reduce.6.cloned.1.call-start = ((), (), s32[]{:S(2)}) async-start(), calls=%async_computation.1 | async-start | bytes 12582912 | tf_op jit(solution)/shard_map/psum | solution.py:171
  128.7 9.6 %collective-permute-start.13 = (bf16[27,256]{1,0:T(8,128)(2,1)S(1)}, bf16[27,256]{1,0:T(8,128)(2,1)S(1)}, u32[]{:S(2)}, u32[]{:S(2)}) collective-permute-start(bf16[27,256]{1,0:T(8,128)(2,1)S(1)} %get-tuple-element.16), channel_id=1, source_target_pairs={{0,2},{2,4},{4,6},{6,8},{8,10},{10,12},{12,14},{14,16},{16,18},{18... | collective-permute-start | bytes 41480 | tf_op jit(solution)/shard_map/ppermute | solution.py:18
  132.2 5.6 %collective-permute-start.12 = (bf16[27,256]{1,0:T(8,128)(2,1)S(1)}, bf16[27,256]{1,0:T(8,128)(2,1)S(1)}, u32[]{:S(2)}, u32[]{:S(2)}) collective-permute-start(bf16[27,256]{1,0:T(8,128)(2,1)S(1)} %get-tuple-element.17), channel_id=1, source_target_pairs={{2,0},{4,2},{6,4},{8,6},{10,8},{12,10},{14,12},{16,14},{18,16},{20... | collective-permute-start | bytes 41480 | tf_op jit(solution)/shard_map/ppermute | solution.py:20
  141.3 6.7 %collective-permute-start.14 = (bf16[9,256]{1,0:T(8,128)(2,1)S(1)}, bf16[9,256]{1,0:T(8,128)(2,1)S(1)}, u32[]{:S(2)}, u32[]{:S(2)}) collective-permute-start(bf16[9,256]{1,0:T(8,128)(2,1)S(1)} %get-tuple-element.15), channel_id=1, source_target_pairs={{2,0},{4,2},{6,4},{8,6},{10,8},{12,10},{14,12},{16,14},{18,16},{20... | collective-permute-start | bytes 13832 | tf_op jit(solution)/shard_map/ppermute | solution.py:20
  144.1 5.7 %collective-permute-start.15 = (bf16[9,256]{1,0:T(8,128)(2,1)S(1)}, bf16[9,256]{1,0:T(8,128)(2,1)S(1)}, u32[]{:S(2)}, u32[]{:S(2)}) collective-permute-start(bf16[9,256]{1,0:T(8,128)(2,1)S(1)} %get-tuple-element.14), channel_id=1, source_target_pairs={{0,2},{2,4},{4,6},{6,8},{8,10},{10,12},{12,14},{14,16},{16,18},{18... | collective-permute-start | bytes 13832 | tf_op jit(solution)/shard_map/ppermute | solution.py:18
  156.5 353.9 %copy-start.34 = (pred[512]{0:T(512)(128)(4,1)S(1)}, pred[512]{0:T(512)(128)(4,1)}, u32[]{:S(2)}) copy-start(pred[512]{0:T(512)(128)(4,1)} %copy-done.33) | copy-start | bytes 1540
  156.5 354.1 %copy-start.32 = (pred[512]{0:T(512)(128)(4,1)S(1)}, pred[512]{0:T(512)(128)(4,1)}, u32[]{:S(2)}) copy-start(pred[512]{0:T(512)(128)(4,1)} %copy-done.31) | copy-start | bytes 1540
  156.5 359.0 %copy-start.51 = (pred[512]{0:T(512)(128)(4,1)S(1)}, pred[512]{0:T(512)(128)(4,1)}, u32[]{:S(2)}) copy-start(pred[512]{0:T(512)(128)(4,1)} %copy-done.49) | copy-start | bytes 1540
  156.6 359.1 %copy-start.48 = (pred[512]{0:T(512)(128)(4,1)S(1)}, pred[512]{0:T(512)(128)(4,1)}, u32[]{:S(2)}) copy-start(pred[512]{0:T(512)(128)(4,1)} %copy-done.46) | copy-start | bytes 1540
  157.2 353.1 %collective-permute-start.16 = (bf16[3,256]{1,0:T(4,128)(2,1)S(1)}, bf16[3,256]{1,0:T(4,128)(2,1)S(1)}, u32[]{:S(2)}, u32[]{:S(2)}) collective-permute-start(bf16[3,256]{1,0:T(4,128)(2,1)S(1)} %get-tuple-element.13), channel_id=1, source_target_pairs={{2,0},{4,2},{6,4},{8,6},{10,8},{12,10},{14,12},{16,14},{18,16},{20... | collective-permute-start | bytes 4616 | tf_op jit(solution)/shard_map/ppermute | solution.py:20
  508.2 7.3 %collective-permute-start.17 = (bf16[3,256]{1,0:T(4,128)(2,1)S(1)}, bf16[3,256]{1,0:T(4,128)(2,1)S(1)}, u32[]{:S(2)}, u32[]{:S(2)}) collective-permute-start(bf16[3,256]{1,0:T(4,128)(2,1)S(1)} %get-tuple-element.12), channel_id=1, source_target_pairs={{0,2},{2,4},{4,6},{6,8},{8,10},{10,12},{12,14},{14,16},{16,18},{18... | collective-permute-start | bytes 4616 | tf_op jit(solution)/shard_map/ppermute | solution.py:18
  (63 other events, 366.4 us)
Sparse Core Ops, SparseCore 0:
  86.9 37.3 all-reduce.3
  156.7 249.6 all-reduce.5
where the time goes:
time: 532 us; the launch traced here: 531 us
  blocking collectives  349 us (66%)
  waiting for transfers between devices  55.9 us (11%)
  starting transfers between devices  51.9 us (10%)
  local copies, waits for them, and re-layouts  22.6 us (4%)
  matrix products  18.8 us (4%)
  other arithmetic  16.8 us (3%)
  between operations  15.8 us (3%)
    psum x1, blocking collectives, shards(): lax.psum((total_a, total_bias, total_b), ('dp', 'seq'))  349 us
    psum x1, waiting for transfers between devices, spread(): return lax.psum(jnp.where(mine, value, jnp.zeros_like(value)), axis)  37.4 us
    ppermute x9, starting transfers between devices, with_halo(): lax.ppermute(tail, axis, [(i, (i + 1) % count) for i in range(ends)])  31.7 us
    ppermute x9, starting transfers between devices, with_halo(): lax.ppermute(head, axis, [((i + 1) % count, i) for i in range(ends)])  20.1 us
    ppermute x9, waiting for transfers between devices, with_halo(): lax.ppermute(head, axis, [((i + 1) % count, i) for i in range(ends)])  11.2 us
    unnamed x160, local copies, waits for them, and re-layouts  11 us
  transfers between devices with their start and end apart: 20, of which 7 were waited for; matrix products, arithmetic and copies ran while one was open for 4% of the time, Pallas kernels for 0%

commit v1 on v0

--- a/solution.py
+++ b/solution.py
@@ -144,7 +144,7 @@
         gate, grad_y = unit_back(unit_idx, grad_y)
         first_gates[unit_idx] = gate
         first_grads[unit_idx] = grad_y
-    latent = spread(grad_y, "segment", 1)
+    latent = lax.ppermute(grad_y, "segment", [(1, 0)])
     grads_a = [None] * UNITS
     grads_bias = [None] * UNITS
     grads_b = [None] * UNITS
@@ -165,10 +165,20 @@
         grads_b[unit_idx] = unit_b
         grad_y = grad_next
     section_grad = jnp.where(is_decoder, first_grads[0], grad_y)
-    total_a = jnp.stack(grads_a)
-    total_bias = jnp.stack(grads_bias)
-    total_b = jnp.stack(grads_b)
-    total_a, total_bias, total_b = lax.psum((total_a, total_bias, total_b), ("dp", "seq"))
+    rows_a = UNITS * KERNEL * channels
+    rows_b = UNITS * inner
+    packed = jnp.concatenate(
+        [
+            jnp.stack(grads_a).reshape(rows_a, inner),
+            jnp.stack(grads_b).reshape(rows_b, channels),
+            jnp.pad(jnp.stack(grads_bias), ((0, 8 - UNITS), (0, 0))),
+        ],
+        axis=0,
+    )
+    packed = lax.psum(packed, ("dp", "seq"))
+    total_a = packed[:rows_a].reshape(UNITS, KERNEL, channels, inner)
+    total_b = packed[rows_a : rows_a + rows_b].reshape(UNITS, inner, channels)
+    total_bias = packed[rows_a + rows_b : rows_a + rows_b + UNITS]
     return (section_grad[None, None], total_a[None], total_bias[None], total_b[None])
 
 

time: 532 us -> 398 us (0.75)
  blocking collectives: 349 us -> 0 us
  waiting for transfers between devices: 55.9 us -> 264 us
  starting transfers between devices: 51.9 us -> 57.5 us
    psum x1 -> x0, blocking collectives: 349 us -> none  [shards(): lax.psum((total_a, total_bias, total_b), ('dp', 'seq'))]
    psum x2 -> x1, waiting for transfers between devices: 37.4 us -> 245 us  [shards(): packed = lax.psum(packed, ('dp', 'seq'))]
    slice x0 -> x3, local copies, waits for them, and re-layouts: none -> 8.12 us  [the longest x1 5.36 us: shards(): total_a = packed[:rows_a].reshape(UNITS, KERNEL, channels, inner)]
    unnamed x160 -> x158, local copies, waits for them, and re-layouts: 11 us -> 3.87 us
  transfers between devices with their start and end apart: 20 -> 20, of which waited for: 7 -> 8; matrix products, arithmetic and copies ran while one was open for 4% -> 5% of each run, Pallas kernels for 0% -> 0%
where the time goes in v1:
time: 398 us; the launch traced here: 395 us
  waiting for transfers between devices  264 us (66%)
  starting transfers between devices  57.5 us (14%)
  local copies, waits for them, and re-layouts  24.1 us (6%)
  matrix products  17.3 us (4%)
  other arithmetic  16.6 us (4%)
  between operations  15.9 us (4%)
    psum x1, waiting for transfers between devices, shards(): packed = lax.psum(packed, ('dp', 'seq'))  245 us
    ppermute x9, starting transfers between devices, with_halo(): lax.ppermute(tail, axis, [(i, (i + 1) % count) for i in range(ends)])  37.1 us
    ppermute x9, starting transfers between devices, with_halo(): lax.ppermute(head, axis, [((i + 1) % count, i) for i in range(ends)])  19.2 us
    ppermute x9, waiting for transfers between devices, with_halo(): lax.ppermute(head, axis, [((i + 1) % count, i) for i in range(ends)])  13.2 us
    unnamed x46, other arithmetic  10.3 us
    transpose x4, local copies, waits for them, and re-layouts, unit_back(): jnp.transpose(weights_a[unit_idx], (0, 2, 1))  9.57 us
  transfers between devices with their start and end apart: 20, of which 8 were waited for; matrix products, arithmetic and copies ran while one was open for 5% of the time, Pallas kernels for 0%

profile of v1, /device:TPU:32, one launch (start us, length us, event | category | flops | bytes accessed | tf_op | source)
XLA Modules:
  0.0 395.1 jit_solution(5626147941762893567)
XLA Ops:
  8.4 3.7 collective-permute-start.1
  12.1 2.1 collective-permute-start
  15.6 3.7 slice_bitcast_fusion.2
  21.9 3.8 collective-permute-start.2
  25.8 2.0 collective-permute-start.3
  28.3 4.1 %collective-permute-done.3 = bf16[9,256]{1,0:T(8,128)(2,1)S(1)} collective-permute-done((bf16[9,256]{1,0:T(8,128)(2,1)S(1)}, bf16[9,256]{1,0:T(8,128)(2,1)S(1)}, u32[]{:S(2)}, u32[]{:S(2)}) %collective-permute-start.3) | collective-permute-done | bytes 4640 | tf_op jit(solution)/shard_map/ppermute | solution.py:20
  34.6 3.9 collective-permute-start.4
  38.5 1.9 collective-permute-start.5
  40.9 4.3 %collective-permute-done.5 = bf16[27,256]{1,0:T(8,128)(2,1)S(1)} collective-permute-done((bf16[27,256]{1,0:T(8,128)(2,1)S(1)}, bf16[27,256]{1,0:T(8,128)(2,1)S(1)}, u32[]{:S(2)}, u32[]{:S(2)}) %collective-permute-start.5) | collective-permute-done | bytes 13856 | tf_op jit(solution)/shard_map/ppermute | solution.py:20
  47.8 1.9 collective-permute-start.6
  49.7 2.3 copy.20
  52.0 4.1 %collective-permute-start.7 = (bf16[27,256]{1,0:T(8,128)(2,1)}, bf16[27,256]{1,0:T(8,128)(2,1)S(1)}, u32[]{:S(2)}, u32[]{:S(2)}) collective-permute-start(bf16[27,256]{1,0:T(8,128)(2,1)} %get-tuple-element.20), channel_id=1, source_target_pairs={{0,2},{2,4},{4,6},{6,8},{8,10},{10,12},{12,14},{14,16},{16,18},{18... | collective-permute-start | bytes 41480 | tf_op jit(solution)/shard_map/ppermute | solution.py:18
  61.3 1.9 collective-permute-start.8
  63.3 2.2 copy.21
  65.5 4.1 %collective-permute-start.9 = (bf16[9,256]{1,0:T(8,128)(2,1)S(1)}, bf16[9,256]{1,0:T(8,128)(2,1)S(1)}, u32[]{:S(2)}, u32[]{:S(2)}) collective-permute-start(bf16[9,256]{1,0:T(8,128)(2,1)S(1)} %get-tuple-element.18), channel_id=1, source_target_pairs={{0,2},{2,4},{4,6},{6,8},{8,10},{10,12},{12,14},{14,16},{16,18},{18... | collective-permute-start | bytes 13832 | tf_op jit(solution)/shard_map/ppermute | solution.py:18
  74.6 1.9 collective-permute-start.10
  77.9 4.4 %collective-permute-start.11 = (bf16[3,256]{1,0:T(4,128)(2,1)}, bf16[3,256]{1,0:T(4,128)(2,1)S(1)}, u32[]{:S(2)}, u32[]{:S(2)}) collective-permute-start(bf16[3,256]{1,0:T(4,128)(2,1)} %get-tuple-element.16), channel_id=1, source_target_pairs={{0,2},{2,4},{4,6},{6,8},{8,10},{10,12},{12,14},{14,16},{16,18},{18... | collective-permute-start | bytes 4616 | tf_op jit(solution)/shard_map/ppermute | solution.py:18
  87.3 2.1 collective-permute-done.12
  89.4 1.5 convert_reduce_fusion
  91.0 2.3 fusion.199
  93.3 5.1 %collective-permute-start.14 = (bf16[27,256]{1,0:T(8,128)(2,1)S(1)}, bf16[27,256]{1,0:T(8,128)(2,1)S(1)}, u32[]{:S(2)}, u32[]{:S(2)}) collective-permute-start(bf16[27,256]{1,0:T(8,128)(2,1)S(1)} %get-tuple-element.14), channel_id=1, source_target_pairs={{0,2},{2,4},{4,6},{6,8},{8,10},{10,12},{12,14},{14,16},{16,18},{18... | collective-permute-start | bytes 41480 | tf_op jit(solution)/shard_map/ppermute | solution.py:18
  98.4 1.9 collective-permute-start.13
  100.8 4.7 %collective-permute-done.13 = bf16[27,256]{1,0:T(8,128)(2,1)S(1)} collective-permute-done((bf16[27,256]{1,0:T(8,128)(2,1)S(1)}, bf16[27,256]{1,0:T(8,128)(2,1)S(1)}, u32[]{:S(2)}, u32[]{:S(2)}) %collective-permute-start.13) | collective-permute-done | bytes 13856 | tf_op jit(solution)/shard_map/ppermute | solution.py:20
  109.0 1.9 collective-permute-start.15
  111.4 4.3 %collective-permute-start.16 = (bf16[9,256]{1,0:T(8,128)(2,1)S(1)}, bf16[9,256]{1,0:T(8,128)(2,1)S(1)}, u32[]{:S(2)}, u32[]{:S(2)}) collective-permute-start(bf16[9,256]{1,0:T(8,128)(2,1)S(1)} %get-tuple-element.12), channel_id=1, source_target_pairs={{0,2},{2,4},{4,6},{6,8},{8,10},{10,12},{12,14},{14,16},{16,18},{18... | collective-permute-start | bytes 13832 | tf_op jit(solution)/shard_map/ppermute | solution.py:18
  120.5 3.1 pad_maximum_fusion
  123.7 1.9 collective-permute-start.17
  125.7 5.3 %collective-permute-start.18 = (bf16[3,256]{1,0:T(4,128)(2,1)S(1)}, bf16[3,256]{1,0:T(4,128)(2,1)S(1)}, u32[]{:S(2)}, u32[]{:S(2)}) collective-permute-start(bf16[3,256]{1,0:T(4,128)(2,1)S(1)} %get-tuple-element.10), channel_id=1, source_target_pairs={{0,2},{2,4},{4,6},{6,8},{8,10},{10,12},{12,14},{14,16},{16,18},{18... | collective-permute-start | bytes 4616 | tf_op jit(solution)/shard_map/ppermute | solution.py:18
  132.7 1.4 fusion.19
  134.1 245.5 %all-reduce.3.cloned.1.call-done = f32[6152,256]{1,0:T(8,128)} async-done(((f32[6152,256]{1,0:T(8,128)}), f32[6152,256]{1,0:T(8,128)}) %all-reduce.3.cloned.1.call-update) | async-done | bytes 6299664 | tf_op jit(solution)/shard_map/psum | solution.py:178
  380.9 2.1 slice.611
  382.9 5.4 %slice.609 = f32[5376,256]{1,0:T(8,128)} slice(f32[6152,256]{1,0:T(8,128)} %all-reduce.3.cloned.1.call-done), slice={[0:5376], [0:256]} | slice | bytes 11010048 | tf_op jit(solution)/shard_map/slice | solution.py:179
  (275 shorter events, 38.4 us)
Async XLA Ops:
  7.2 372.4 %all-reduce.3.cloned.1.call-start = ((), (), s32[]{:S(2)}) async-start(), calls=%async_computation | async-start | bytes 12599296 | tf_op jit(solution)/shard_map/psum | solution.py:178
  8.4 11.6 %collective-permute-start.1 = (bf16[3,256]{1,0:T(4,128)(2,1)S(1)}, bf16[3,256]{1,0:T(4,128)(2,1)S(1)}, u32[]{:S(2)}, u32[]{:S(2)}) collective-permute-start(bf16[3,256]{1,0:T(4,128)(2,1)S(1)} %get-tuple-element.26), channel_id=1, source_target_pairs={{2,0},{4,2},{6,4},{8,6},{10,8},{12,10},{14,12},{16,14},{18,16},{20... | collective-permute-start | bytes 4616 | tf_op jit(solution)/shard_map/ppermute | solution.py:20
  12.1 7.2 %collective-permute-start = (bf16[3,256]{1,0:T(4,128)(2,1)S(1)}, bf16[3,256]{1,0:T(4,128)(2,1)S(1)}, u32[]{:S(2)}, u32[]{:S(2)}) collective-permute-start(bf16[3,256]{1,0:T(4,128)(2,1)S(1)} %get-tuple-element.27), channel_id=1, source_target_pairs={{0,2},{2,4},{4,6},{6,8},{8,10},{10,12},{12,14},{14,16},{16,18},{18... | collective-permute-start | bytes 4616 | tf_op jit(solution)/shard_map/ppermute | solution.py:18
  15.4 12.7 %copy-start.28 = (pred[512]{0:T(512)(128)(4,1)}, pred[512]{0:T(512)(128)(4,1)S(1)}, u32[]{:S(2)}) copy-start(pred[512]{0:T(512)(128)(4,1)S(1)} %get-tuple-element.40) | copy-start | bytes 1540
  15.4 25.0 %copy-start.51 = (pred[512]{0:T(512)(128)(4,1)}, pred[512]{0:T(512)(128)(4,1)S(1)}, u32[]{:S(2)}) copy-start(pred[512]{0:T(512)(128)(4,1)S(1)} %get-tuple-element.41) | copy-start | bytes 1540
  15.4 30.0 %copy-start.54 = (pred[512]{0:T(512)(128)(4,1)}, pred[512]{0:T(512)(128)(4,1)S(1)}, u32[]{:S(2)}) copy-start(pred[512]{0:T(512)(128)(4,1)S(1)} %get-tuple-element.37) | copy-start | bytes 1540
  15.5 16.9 %copy-start.21 = (pred[512]{0:T(512)(128)(4,1)}, pred[512]{0:T(512)(128)(4,1)S(1)}, u32[]{:S(2)}) copy-start(pred[512]{0:T(512)(128)(4,1)S(1)} %get-tuple-element.34) | copy-start | bytes 1540
  15.5 17.0 %copy-start.37 = (pred[512]{0:T(512)(128)(4,1)}, pred[512]{0:T(512)(128)(4,1)S(1)}, u32[]{:S(2)}) copy-start(pred[512]{0:T(512)(128)(4,1)S(1)} %get-tuple-element.31) | copy-start | bytes 1540
  15.5 25.0 %copy-start.40 = (pred[512]{0:T(512)(128)(4,1)}, pred[512]{0:T(512)(128)(4,1)S(1)}, u32[]{:S(2)}) copy-start(pred[512]{0:T(512)(128)(4,1)S(1)} %get-tuple-element.29) | copy-start | bytes 1540
  15.5 25.2 %copy-start.23 = (pred[512]{0:T(512)(128)(4,1)}, pred[512]{0:T(512)(128)(4,1)S(1)}, u32[]{:S(2)}) copy-start(pred[512]{0:T(512)(128)(4,1)S(1)} %get-tuple-element.33) | copy-start | bytes 1540
  15.6 29.7 %copy-start.26 = (pred[512]{0:T(512)(128)(4,1)}, pred[512]{0:T(512)(128)(4,1)S(1)}, u32[]{:S(2)}) copy-start(pred[512]{0:T(512)(128)(4,1)S(1)} %get-tuple-element.30) | copy-start | bytes 1540
  15.6 30.0 %copy-start.43 = (pred[512]{0:T(512)(128)(4,1)}, pred[512]{0:T(512)(128)(4,1)S(1)}, u32[]{:S(2)}) copy-start(pred[512]{0:T(512)(128)(4,1)S(1)} %get-tuple-element.28) | copy-start | bytes 1540
  21.9 5.9 %collective-permute-start.2 = (bf16[9,256]{1,0:T(8,128)(2,1)S(1)}, bf16[9,256]{1,0:T(8,128)(2,1)S(1)}, u32[]{:S(2)}, u32[]{:S(2)}) collective-permute-start(bf16[9,256]{1,0:T(8,128)(2,1)S(1)} %get-tuple-element.25), channel_id=1, source_target_pairs={{0,2},{2,4},{4,6},{6,8},{8,10},{10,12},{12,14},{14,16},{16,18},{18... | collective-permute-start | bytes 13832 | tf_op jit(solution)/shard_map/ppermute | solution.py:18
  25.8 6.7 %collective-permute-start.3 = (bf16[9,256]{1,0:T(8,128)(2,1)S(1)}, bf16[9,256]{1,0:T(8,128)(2,1)S(1)}, u32[]{:S(2)}, u32[]{:S(2)}) collective-permute-start(bf16[9,256]{1,0:T(8,128)(2,1)S(1)} %get-tuple-element.24), channel_id=1, source_target_pairs={{2,0},{4,2},{6,4},{8,6},{10,8},{12,10},{14,12},{16,14},{18,16},{20... | collective-permute-start | bytes 13832 | tf_op jit(solution)/shard_map/ppermute | solution.py:20
  34.5 24.4 %copy-start.17 = (f32[512,256]{1,0:T(8,128)}, f32[512,256]{1,0:T(8,128)S(1)}, u32[]{:S(2)}) copy-start(f32[512,256]{1,0:T(8,128)S(1)} %get-tuple-element.48) | copy-start | bytes 1572868
  34.6 5.9 %collective-permute-start.4 = (bf16[27,256]{1,0:T(8,128)(2,1)S(1)}, bf16[27,256]{1,0:T(8,128)(2,1)S(1)}, u32[]{:S(2)}, u32[]{:S(2)}) collective-permute-start(bf16[27,256]{1,0:T(8,128)(2,1)S(1)} %get-tuple-element.23), channel_id=1, source_target_pairs={{0,2},{2,4},{4,6},{6,8},{8,10},{10,12},{12,14},{14,16},{16,18},{18... | collective-permute-start | bytes 41480 | tf_op jit(solution)/shard_map/ppermute | solution.py:18
  38.5 6.7 %collective-permute-start.5 = (bf16[27,256]{1,0:T(8,128)(2,1)S(1)}, bf16[27,256]{1,0:T(8,128)(2,1)S(1)}, u32[]{:S(2)}, u32[]{:S(2)}) collective-permute-start(bf16[27,256]{1,0:T(8,128)(2,1)S(1)} %get-tuple-element.22), channel_id=1, source_target_pairs={{2,0},{4,2},{6,4},{8,6},{10,8},{12,10},{14,12},{16,14},{18,16},{20... | collective-permute-start | bytes 41480 | tf_op jit(solution)/shard_map/ppermute | solution.py:20
  47.8 8.3 %collective-permute-start.6 = (bf16[27,256]{1,0:T(8,128)(2,1)}, bf16[27,256]{1,0:T(8,128)(2,1)S(1)}, u32[]{:S(2)}, u32[]{:S(2)}) collective-permute-start(bf16[27,256]{1,0:T(8,128)(2,1)} %get-tuple-element.21), channel_id=1, source_target_pairs={{2,0},{4,2},{6,4},{8,6},{10,8},{12,10},{14,12},{16,14},{18,16},{20... | collective-permute-start | bytes 41480 | tf_op jit(solution)/shard_map/ppermute | solution.py:20
  52.0 6.4 %collective-permute-start.7 = (bf16[27,256]{1,0:T(8,128)(2,1)}, bf16[27,256]{1,0:T(8,128)(2,1)S(1)}, u32[]{:S(2)}, u32[]{:S(2)}) collective-permute-start(bf16[27,256]{1,0:T(8,128)(2,1)} %get-tuple-element.20), channel_id=1, source_target_pairs={{0,2},{2,4},{4,6},{6,8},{8,10},{10,12},{12,14},{14,16},{16,18},{18... | collective-permute-start | bytes 41480 | tf_op jit(solution)/shard_map/ppermute | solution.py:18
  61.3 8.3 %collective-permute-start.8 = (bf16[9,256]{1,0:T(8,128)(2,1)S(1)}, bf16[9,256]{1,0:T(8,128)(2,1)S(1)}, u32[]{:S(2)}, u32[]{:S(2)}) collective-permute-start(bf16[9,256]{1,0:T(8,128)(2,1)S(1)} %get-tuple-element.19), channel_id=1, source_target_pairs={{2,0},{4,2},{6,4},{8,6},{10,8},{12,10},{14,12},{16,14},{18,16},{20... | collective-permute-start | bytes 13832 | tf_op jit(solution)/shard_map/ppermute | solution.py:20
  65.5 5.7 %collective-permute-start.9 = (bf16[9,256]{1,0:T(8,128)(2,1)S(1)}, bf16[9,256]{1,0:T(8,128)(2,1)S(1)}, u32[]{:S(2)}, u32[]{:S(2)}) collective-permute-start(bf16[9,256]{1,0:T(8,128)(2,1)S(1)} %get-tuple-element.18), channel_id=1, source_target_pairs={{0,2},{2,4},{4,6},{6,8},{8,10},{10,12},{12,14},{14,16},{16,18},{18... | collective-permute-start | bytes 13832 | tf_op jit(solution)/shard_map/ppermute | solution.py:18
  74.6 7.7 %collective-permute-start.10 = (bf16[3,256]{1,0:T(4,128)(2,1)}, bf16[3,256]{1,0:T(4,128)(2,1)}, u32[]{:S(2)}, u32[]{:S(2)}) collective-permute-start(bf16[3,256]{1,0:T(4,128)(2,1)} %get-tuple-element.17), channel_id=1, source_target_pairs={{2,0},{4,2},{6,4},{8,6},{10,8},{12,10},{14,12},{16,14},{18,16},{20... | collective-permute-start | bytes 4616 | tf_op jit(solution)/shard_map/ppermute | solution.py:20
  77.9 6.9 %collective-permute-start.11 = (bf16[3,256]{1,0:T(4,128)(2,1)}, bf16[3,256]{1,0:T(4,128)(2,1)S(1)}, u32[]{:S(2)}, u32[]{:S(2)}) collective-permute-start(bf16[3,256]{1,0:T(4,128)(2,1)} %get-tuple-element.16), channel_id=1, source_target_pairs={{0,2},{2,4},{4,6},{6,8},{8,10},{10,12},{12,14},{14,16},{16,18},{18... | collective-permute-start | bytes 4616 | tf_op jit(solution)/shard_map/ppermute | solution.py:18
  86.0 3.4 collective-permute-start.12
  91.0 14.6 %copy-start.44 = (pred[512]{0:T(512)(128)(4,1)S(1)}, pred[512]{0:T(512)(128)(4,1)}, u32[]{:S(2)}) copy-start(pred[512]{0:T(512)(128)(4,1)} %copy-done.43) | copy-start | bytes 1540
  93.3 12.4 %copy-start.55 = (pred[512]{0:T(512)(128)(4,1)S(1)}, pred[512]{0:T(512)(128)(4,1)}, u32[]{:S(2)}) copy-start(pred[512]{0:T(512)(128)(4,1)} %copy-done.54) | copy-start | bytes 1540
  93.3 12.7 %collective-permute-start.14 = (bf16[27,256]{1,0:T(8,128)(2,1)S(1)}, bf16[27,256]{1,0:T(8,128)(2,1)S(1)}, u32[]{:S(2)}, u32[]{:S(2)}) collective-permute-start(bf16[27,256]{1,0:T(8,128)(2,1)S(1)} %get-tuple-element.14), channel_id=1, source_target_pairs={{0,2},{2,4},{4,6},{6,8},{8,10},{10,12},{12,14},{14,16},{16,18},{18... | collective-permute-start | bytes 41480 | tf_op jit(solution)/shard_map/ppermute | solution.py:18
  98.4 7.1 %collective-permute-start.13 = (bf16[27,256]{1,0:T(8,128)(2,1)S(1)}, bf16[27,256]{1,0:T(8,128)(2,1)S(1)}, u32[]{:S(2)}, u32[]{:S(2)}) collective-permute-start(bf16[27,256]{1,0:T(8,128)(2,1)S(1)} %get-tuple-element.15), channel_id=1, source_target_pairs={{2,0},{4,2},{6,4},{8,6},{10,8},{12,10},{14,12},{16,14},{18,16},{20... | collective-permute-start | bytes 41480 | tf_op jit(solution)/shard_map/ppermute | solution.py:20
  109.0 6.7 %collective-permute-start.15 = (bf16[9,256]{1,0:T(8,128)(2,1)S(1)}, bf16[9,256]{1,0:T(8,128)(2,1)S(1)}, u32[]{:S(2)}, u32[]{:S(2)}) collective-permute-start(bf16[9,256]{1,0:T(8,128)(2,1)S(1)} %get-tuple-element.13), channel_id=1, source_target_pairs={{2,0},{4,2},{6,4},{8,6},{10,8},{12,10},{14,12},{16,14},{18,16},{20... | collective-permute-start | bytes 13832 | tf_op jit(solution)/shard_map/ppermute | solution.py:20
  111.4 5.7 %collective-permute-start.16 = (bf16[9,256]{1,0:T(8,128)(2,1)S(1)}, bf16[9,256]{1,0:T(8,128)(2,1)S(1)}, u32[]{:S(2)}, u32[]{:S(2)}) collective-permute-start(bf16[9,256]{1,0:T(8,128)(2,1)S(1)} %get-tuple-element.12), channel_id=1, source_target_pairs={{0,2},{2,4},{4,6},{6,8},{8,10},{10,12},{12,14},{14,16},{16,18},{18... | collective-permute-start | bytes 13832 | tf_op jit(solution)/shard_map/ppermute | solution.py:18
  123.7 7.2 %collective-permute-start.17 = (bf16[3,256]{1,0:T(4,128)(2,1)S(1)}, bf16[3,256]{1,0:T(4,128)(2,1)S(1)}, u32[]{:S(2)}, u32[]{:S(2)}) collective-permute-start(bf16[3,256]{1,0:T(4,128)(2,1)S(1)} %get-tuple-element.11), channel_id=1, source_target_pairs={{2,0},{4,2},{6,4},{8,6},{10,8},{12,10},{14,12},{16,14},{18,16},{20... | collective-permute-start | bytes 4616 | tf_op jit(solution)/shard_map/ppermute | solution.py:20
  125.7 6.6 %collective-permute-start.18 = (bf16[3,256]{1,0:T(4,128)(2,1)S(1)}, bf16[3,256]{1,0:T(4,128)(2,1)S(1)}, u32[]{:S(2)}, u32[]{:S(2)}) collective-permute-start(bf16[3,256]{1,0:T(4,128)(2,1)S(1)} %get-tuple-element.10), channel_id=1, source_target_pairs={{0,2},{2,4},{4,6},{6,8},{8,10},{10,12},{12,14},{14,16},{16,18},{18... | collective-permute-start | bytes 4616 | tf_op jit(solution)/shard_map/ppermute | solution.py:18
  (63 other events, 365.1 us)
Sparse Core Ops, SparseCore 0:
  123.8 255.7 all-reduce.2

commit v2 on v1

--- a/solution.py
+++ b/solution.py
@@ -175,7 +175,14 @@
         ],
         axis=0,
     )
-    packed = lax.psum(packed, ("dp", "seq"))
+    group = lax.axis_size("dp") * lax.axis_size("seq")
+    rows = packed.shape[0]
+    share = -(-rows // (group * 8)) * 8
+    packed = jnp.pad(packed, ((0, share * group - rows), (0, 0)))
+    packed = lax.psum_scatter(packed, ("dp", "seq"), scatter_dimension=0, tiled=True)
+    packed = lax.all_gather(
+        packed.astype(jnp.bfloat16), ("dp", "seq"), axis=0, tiled=True
+    ).astype(jnp.float32)
     total_a = packed[:rows_a].reshape(UNITS, KERNEL, channels, inner)
     total_b = packed[rows_a : rows_a + rows_b].reshape(UNITS, inner, channels)
     total_bias = packed[rows_a + rows_b : rows_a + rows_b + UNITS]

time: 398 us -> 1520 us (3.82)
  waiting for transfers between devices: 264 us -> 1380 us
    reduce_scatter x0 -> x1, waiting for transfers between devices: none -> 722 us  [shards(): lax.psum_scatter(packed, ('dp', 'seq'), scatter_dimension=0, tiled=True)]
    all_gather x0 -> x1, waiting for transfers between devices: none -> 638 us  [shards(): lax.all_gather(packed.astype(jnp.bfloat16), ('dp', 'seq'), axis=0, tiled=...]
    psum x1 -> x0, waiting for transfers between devices: 245 us -> none  [shards(): packed = lax.psum(packed, ('dp', 'seq'))]
  transfers between devices with their start and end apart: 20 -> 21, of which waited for: 8 -> 9; matrix products, arithmetic and copies ran while one was open for 5% -> 1% of each run, Pallas kernels for 0% -> 0%
where the time goes in v2:
time: 1520 us
  waiting for transfers between devices  1380 us (91%)
  starting transfers between devices  60.3 us (4%)
  local copies, waits for them, and re-layouts  23.3 us (2%)
  other arithmetic  18.5 us (1%)
  matrix products  17.3 us (1%)
  between operations  15.9 us (1%)
    reduce_scatter x1, waiting for transfers between devices, shards(): lax.psum_scatter(packed, ('dp', 'seq'), scatter_dimension=0, tiled=True)  722 us
    all_gather x1, waiting for transfers between devices, shards(): lax.all_gather(packed.astype(jnp.bfloat16), ('dp', 'seq'), axis=0, tiled=...  638 us
    ppermute x9, starting transfers between devices, with_halo(): lax.ppermute(tail, axis, [(i, (i + 1) % count) for i in range(ends)])  33.9 us
  transfers between devices with their start and end apart: 21, of which 9 were waited for; matrix products, arithmetic and copies ran while one was open for 1% of the time, Pallas kernels for 0%

profile of v2, /device:TPU:32, one launch (start us, length us, event | category | flops | bytes accessed | tf_op | source)
XLA Modules:
  0.0 1515.7 jit_solution(5419906882155847757)
XLA Ops:
  8.4 3.7 collective-permute-start.1
  12.1 2.1 collective-permute-start
  15.6 3.7 slice_bitcast_fusion.2
  21.9 3.8 collective-permute-start.2
  25.8 2.0 collective-permute-start.3
  28.3 4.1 collective-permute-done.3
  34.6 3.9 collective-permute-start.4
  38.5 1.9 collective-permute-start.5
  40.9 4.3 collective-permute-done.5
  47.8 1.9 collective-permute-start.6
  49.7 2.2 copy.20
  52.0 4.1 collective-permute-start.7
  61.4 1.9 collective-permute-start.8
  63.3 2.2 copy.21
  65.6 4.1 collective-permute-start.9
  74.7 1.9 collective-permute-start.10
  78.0 4.4 collective-permute-start.11
  87.4 2.1 collective-permute-done.12
  91.1 2.3 fusion.199
  93.4 5.1 collective-permute-start.14
  98.5 1.9 collective-permute-start.13
  100.9 4.7 collective-permute-done.13
  109.1 1.9 collective-permute-start.15
  111.5 4.3 collective-permute-start.16
  120.8 3.3 select_maximum_fusion
  124.2 722.4 %reduce-scatter.2.cloned.1.call-done = f32[56,256]{1,0:T(8,128)} async-done(((f32[7168,256]{1,0:T(8,128)}), f32[56,256]{1,0:T(8,128)}) %reduce-scatter.2.cloned.1.call-update) | async-done | bytes 57360 | tf_op jit(solution)/shard_map/reduce_scatter | solution.py:182
  848.0 7.8 collective-permute-start.17
  855.9 2.1 collective-permute-start.18
  858.4 3.1 collective-permute-done.18
  863.4 637.6 %all-gather.2.cloned.1.call-done = bf16[7168,256]{1,0:T(8,128)(2,1)} async-done(((bf16[56,256]{1,0:T(8,128)(2,1)}), bf16[7168,256]{1,0:T(8,128)(2,1)}) %all-gather.2.cloned.1.call-update) | async-done | bytes 3670032 | tf_op jit(solution)/shard_map/all_gather | solution.py:183
  1502.3 1.9 slice.611
  1504.2 4.7 slice.609
  (279 shorter events, 42.3 us)
Async XLA Ops:
  7.2 839.4 %reduce-scatter.2.cloned.1.call-start = ((), (), s32[]{:S(2)}) async-start(), calls=%async_computation.1 | async-start | bytes 7397376 | tf_op jit(solution)/shard_map/reduce_scatter | solution.py:182
  8.4 11.6 collective-permute-start.1
  12.1 7.2 collective-permute-start
  15.4 25.1 %copy-start.51 = (pred[512]{0:T(512)(128)(4,1)}, pred[512]{0:T(512)(128)(4,1)S(1)}, u32[]{:S(2)}) copy-start(pred[512]{0:T(512)(128)(4,1)S(1)} %get-tuple-element.41) | copy-start | bytes 1540
  15.4 30.0 %copy-start.54 = (pred[512]{0:T(512)(128)(4,1)}, pred[512]{0:T(512)(128)(4,1)S(1)}, u32[]{:S(2)}) copy-start(pred[512]{0:T(512)(128)(4,1)S(1)} %get-tuple-element.37) | copy-start | bytes 1540
  15.5 25.1 %copy-start.40 = (pred[512]{0:T(512)(128)(4,1)}, pred[512]{0:T(512)(128)(4,1)S(1)}, u32[]{:S(2)}) copy-start(pred[512]{0:T(512)(128)(4,1)S(1)} %get-tuple-element.29) | copy-start | bytes 1540
  15.5 25.2 %copy-start.23 = (pred[512]{0:T(512)(128)(4,1)}, pred[512]{0:T(512)(128)(4,1)S(1)}, u32[]{:S(2)}) copy-start(pred[512]{0:T(512)(128)(4,1)S(1)} %get-tuple-element.33) | copy-start | bytes 1540
  15.6 29.7 %copy-start.26 = (pred[512]{0:T(512)(128)(4,1)}, pred[512]{0:T(512)(128)(4,1)S(1)}, u32[]{:S(2)}) copy-start(pred[512]{0:T(512)(128)(4,1)S(1)} %get-tuple-element.30) | copy-start | bytes 1540
  15.6 30.0 %copy-start.43 = (pred[512]{0:T(512)(128)(4,1)}, pred[512]{0:T(512)(128)(4,1)S(1)}, u32[]{:S(2)}) copy-start(pred[512]{0:T(512)(128)(4,1)S(1)} %get-tuple-element.28) | copy-start | bytes 1540
  21.9 5.9 collective-permute-start.2
  25.8 6.7 collective-permute-start.3
  34.5 24.4 %copy-start.17 = (f32[512,256]{1,0:T(8,128)}, f32[512,256]{1,0:T(8,128)S(1)}, u32[]{:S(2)}) copy-start(f32[512,256]{1,0:T(8,128)S(1)} %get-tuple-element.48) | copy-start | bytes 1572868
  34.6 5.9 collective-permute-start.4
  38.5 6.7 collective-permute-start.5
  47.8 8.2 collective-permute-start.6
  52.0 6.5 collective-permute-start.7
  61.4 8.3 collective-permute-start.8
  65.6 5.7 collective-permute-start.9
  74.7 7.7 collective-permute-start.10
  78.0 6.9 collective-permute-start.11
  86.1 3.4 collective-permute-start.12
  93.4 12.7 collective-permute-start.14
  98.5 7.1 collective-permute-start.13
  109.1 6.7 collective-permute-start.15
  111.5 5.7 collective-permute-start.16
  124.1 734.0 %copy-start.33 = (pred[512]{0:T(512)(128)(4,1)S(1)}, pred[512]{0:T(512)(128)(4,1)}, u32[]{:S(2)}) copy-start(pred[512]{0:T(512)(128)(4,1)} %copy-done.32) | copy-start | bytes 1540
  124.1 734.2 %copy-start.31 = (pred[512]{0:T(512)(128)(4,1)S(1)}, pred[512]{0:T(512)(128)(4,1)}, u32[]{:S(2)}) copy-start(pred[512]{0:T(512)(128)(4,1)} %copy-done.30) | copy-start | bytes 1540
  124.1 737.4 %copy-start.50 = (pred[512]{0:T(512)(128)(4,1)S(1)}, pred[512]{0:T(512)(128)(4,1)}, u32[]{:S(2)}) copy-start(pred[512]{0:T(512)(128)(4,1)} %copy-done.48) | copy-start | bytes 1540
  124.1 737.5 %copy-start.47 = (pred[512]{0:T(512)(128)(4,1)S(1)}, pred[512]{0:T(512)(128)(4,1)}, u32[]{:S(2)}) copy-start(pred[512]{0:T(512)(128)(4,1)} %copy-done.45) | copy-start | bytes 1540
  124.1 1376.9 %all-gather.2.cloned.1.call-start = ((), (), s32[]{:S(2)}) async-start(), calls=%async_computation.2 | async-start | bytes 3698688 | tf_op jit(solution)/shard_map/all_gather | solution.py:183
  848.0 9.9 collective-permute-start.17
  855.9 5.6 collective-permute-start.18
  (64 other events, 405.4 us)
Sparse Core Ops, SparseCore 0:
  124.2 722.2 reduce-scatter.1
  848.9 652.0 all-gather.1

commit v3 on v1

--- a/solution.py
+++ b/solution.py
@@ -175,7 +175,7 @@
         ],
         axis=0,
     )
-    packed = lax.psum(packed, ("dp", "seq"))
+    packed = lax.psum(packed.astype(jnp.bfloat16), ("dp", "seq")).astype(jnp.float32)
     total_a = packed[:rows_a].reshape(UNITS, KERNEL, channels, inner)
     total_b = packed[rows_a : rows_a + rows_b].reshape(UNITS, inner, channels)
     total_bias = packed[rows_a + rows_b : rows_a + rows_b + UNITS]

time: 398 us -> 394 us (0.990)
  waiting for transfers between devices: 264 us -> 258 us
    psum x1, waiting for transfers between devices: 245 us -> 240 us  [shards(): lax.psum(packed.astype(jnp.bfloat16), ('dp', 'seq')).astype(jnp.float32)]
    transpose x4, local copies, waits for them, and re-layouts: 9.57 us -> 5.06 us  [unit_back(): jnp.transpose(weights_a[unit_idx], (0, 2, 1))]
    unnamed x46 -> x43, other arithmetic: 10.3 us -> 12.8 us
  transfers between devices with their start and end apart: 20 -> 20, of which waited for: 8 -> 7; matrix products, arithmetic and copies ran while one was open for 5% -> 6% of each run, Pallas kernels for 0% -> 0%
where the time goes in v3:
time: 394 us; the launch traced here: 391 us
  waiting for transfers between devices  258 us (65%)
  starting transfers between devices  57.3 us (15%)
  local copies, waits for them, and re-layouts  21.9 us (6%)
  other arithmetic  19.8 us (5%)
  matrix products  18.7 us (5%)
  between operations  15.8 us (4%)
    psum x1, waiting for transfers between devices, shards(): lax.psum(packed.astype(jnp.bfloat16), ('dp', 'seq')).astype(jnp.float32)  240 us
    ppermute x9, starting transfers between devices, with_halo(): lax.ppermute(tail, axis, [(i, (i + 1) % count) for i in range(ends)])  36.8 us
    ppermute x9, starting transfers between devices, with_halo(): lax.ppermute(head, axis, [((i + 1) % count, i) for i in range(ends)])  19.2 us
    ppermute x9, waiting for transfers between devices, with_halo(): lax.ppermute(head, axis, [((i + 1) % count, i) for i in range(ends)])  13.2 us
    unnamed x43, other arithmetic  12.8 us
  transfers between devices with their start and end apart: 20, of which 7 were waited for; matrix products, arithmetic and copies ran while one was open for 6% of the time, Pallas kernels for 0%

profile of v3, /device:TPU:32, one launch (start us, length us, event | category | flops | bytes accessed | tf_op | source)
XLA Modules:
  0.0 390.9 jit_solution(4766512363003614145)
XLA Ops:
  8.4 3.7 collective-permute-start.1
  12.1 2.1 collective-permute-start
  15.6 2.4 slice_bitcast_fusion.2
  21.0 3.8 collective-permute-start.2
  24.8 2.0 collective-permute-start.3
  27.3 4.1 %collective-permute-done.3 = bf16[9,256]{1,0:T(8,128)(2,1)S(1)} collective-permute-done((bf16[9,256]{1,0:T(8,128)(2,1)S(1)}, bf16[9,256]{1,0:T(8,128)(2,1)S(1)}, u32[]{:S(2)}, u32[]{:S(2)}) %collective-permute-start.3) | collective-permute-done | bytes 4640 | tf_op jit(solution)/shard_map/ppermute | solution.py:20
  33.7 3.9 %collective-permute-start.4 = (bf16[27,256]{1,0:T(8,128)(2,1)S(1)}, bf16[27,256]{1,0:T(8,128)(2,1)S(1)}, u32[]{:S(2)}, u32[]{:S(2)}) collective-permute-start(bf16[27,256]{1,0:T(8,128)(2,1)S(1)} %get-tuple-element.29), channel_id=1, source_target_pairs={{0,2},{2,4},{4,6},{6,8},{8,10},{10,12},{12,14},{14,16},{16,18},{18... | collective-permute-start | bytes 41480 | tf_op jit(solution)/shard_map/ppermute | solution.py:18
  37.6 1.9 collective-permute-start.5
  40.0 4.3 %collective-permute-done.5 = bf16[27,256]{1,0:T(8,128)(2,1)S(1)} collective-permute-done((bf16[27,256]{1,0:T(8,128)(2,1)S(1)}, bf16[27,256]{1,0:T(8,128)(2,1)S(1)}, u32[]{:S(2)}, u32[]{:S(2)}) %collective-permute-start.5) | collective-permute-done | bytes 13856 | tf_op jit(solution)/shard_map/ppermute | solution.py:20
  46.9 1.9 collective-permute-start.6
  48.8 1.4 copy.20
  50.2 4.1 %collective-permute-start.7 = (bf16[27,256]{1,0:T(8,128)(2,1)}, bf16[27,256]{1,0:T(8,128)(2,1)S(1)}, u32[]{:S(2)}, u32[]{:S(2)}) collective-permute-start(bf16[27,256]{1,0:T(8,128)(2,1)} %get-tuple-element.26), channel_id=1, source_target_pairs={{0,2},{2,4},{4,6},{6,8},{8,10},{10,12},{12,14},{14,16},{16,18},{18... | collective-permute-start | bytes 41480 | tf_op jit(solution)/shard_map/ppermute | solution.py:18
  59.4 1.9 collective-permute-start.8
  62.0 4.1 %collective-permute-start.9 = (bf16[9,256]{1,0:T(8,128)(2,1)S(1)}, bf16[9,256]{1,0:T(8,128)(2,1)S(1)}, u32[]{:S(2)}, u32[]{:S(2)}) collective-permute-start(bf16[9,256]{1,0:T(8,128)(2,1)S(1)} %get-tuple-element.24), channel_id=1, source_target_pairs={{0,2},{2,4},{4,6},{6,8},{8,10},{10,12},{12,14},{14,16},{16,18},{18... | collective-permute-start | bytes 13832 | tf_op jit(solution)/shard_map/ppermute | solution.py:18
  71.1 1.9 collective-permute-start.10
  73.7 4.4 %collective-permute-start.11 = (bf16[3,256]{1,0:T(4,128)(2,1)}, bf16[3,256]{1,0:T(4,128)(2,1)S(1)}, u32[]{:S(2)}, u32[]{:S(2)}) collective-permute-start(bf16[3,256]{1,0:T(4,128)(2,1)} %get-tuple-element.22), channel_id=1, source_target_pairs={{0,2},{2,4},{4,6},{6,8},{8,10},{10,12},{12,14},{14,16},{16,18},{18... | collective-permute-start | bytes 4616 | tf_op jit(solution)/shard_map/ppermute | solution.py:18
  81.7 1.3 collective-permute-start.12
  83.0 2.1 collective-permute-done.12
  85.2 1.5 fusion.15
  86.7 2.3 convolution_convert_fusion
  89.0 5.1 %collective-permute-start.14 = (bf16[27,256]{1,0:T(8,128)(2,1)S(1)}, bf16[27,256]{1,0:T(8,128)(2,1)S(1)}, u32[]{:S(2)}, u32[]{:S(2)}) collective-permute-start(bf16[27,256]{1,0:T(8,128)(2,1)S(1)} %get-tuple-element.20), channel_id=1, source_target_pairs={{0,2},{2,4},{4,6},{6,8},{8,10},{10,12},{12,14},{14,16},{16,18},{18... | collective-permute-start | bytes 41480 | tf_op jit(solution)/shard_map/ppermute | solution.py:18
  94.1 1.9 collective-permute-start.13
  96.5 4.7 %collective-permute-done.13 = bf16[27,256]{1,0:T(8,128)(2,1)S(1)} collective-permute-done((bf16[27,256]{1,0:T(8,128)(2,1)S(1)}, bf16[27,256]{1,0:T(8,128)(2,1)S(1)}, u32[]{:S(2)}, u32[]{:S(2)}) %collective-permute-start.13) | collective-permute-done | bytes 13856 | tf_op jit(solution)/shard_map/ppermute | solution.py:20
  105.2 1.9 collective-permute-start.15
  107.6 4.2 %collective-permute-start.16 = (bf16[9,256]{1,0:T(8,128)(2,1)S(1)}, bf16[9,256]{1,0:T(8,128)(2,1)S(1)}, u32[]{:S(2)}, u32[]{:S(2)}) collective-permute-start(bf16[9,256]{1,0:T(8,128)(2,1)S(1)} %get-tuple-element.18), channel_id=1, source_target_pairs={{0,2},{2,4},{4,6},{6,8},{8,10},{10,12},{12,14},{14,16},{16,18},{18... | collective-permute-start | bytes 13832 | tf_op jit(solution)/shard_map/ppermute | solution.py:18
  117.1 1.9 collective-permute-start.17
  119.4 5.1 %collective-permute-start.18 = (bf16[3,256]{1,0:T(4,128)(2,1)S(1)}, bf16[3,256]{1,0:T(4,128)(2,1)S(1)}, u32[]{:S(2)}, u32[]{:S(2)}) collective-permute-start(bf16[3,256]{1,0:T(4,128)(2,1)S(1)} %get-tuple-element.16), channel_id=1, source_target_pairs={{0,2},{2,4},{4,6},{6,8},{8,10},{10,12},{12,14},{14,16},{16,18},{18... | collective-permute-start | bytes 4616 | tf_op jit(solution)/shard_map/ppermute | solution.py:18
  128.9 1.9 pad_maximum_fusion
  133.1 2.9 fusion.19
  136.0 240.2 %all-reduce.3.cloned.1.call-done = bf16[6152,256]{1,0:T(8,128)(2,1)} async-done(((bf16[6152,256]{1,0:T(8,128)(2,1)}), bf16[6152,256]{1,0:T(8,128)(2,1)}) %all-reduce.3.cloned.1.call-update) | async-done | bytes 3149840 | tf_op jit(solution)/shard_map/psum | solution.py:178
  377.5 1.9 slice.611
  379.4 4.7 %slice.609 = f32[5376,256]{1,0:T(8,128)} slice(bf16[6152,256]{1,0:T(8,128)(2,1)} %all-reduce.3.cloned.1.call-done), slice={[0:5376], [0:256]} | slice | bytes 11010048 | tf_op jit(solution)/shard_map/slice | solution.py:179
  (278 shorter events, 43.5 us)
Async XLA Ops:
  7.2 369.0 %all-reduce.3.cloned.1.call-start = ((), (), s32[]{:S(2)}) async-start(), calls=%async_computation | async-start | bytes 6299648 | tf_op jit(solution)/shard_map/psum | solution.py:178
  8.4 10.4 %collective-permute-start.1 = (bf16[3,256]{1,0:T(4,128)(2,1)S(1)}, bf16[3,256]{1,0:T(4,128)(2,1)S(1)}, u32[]{:S(2)}, u32[]{:S(2)}) collective-permute-start(bf16[3,256]{1,0:T(4,128)(2,1)S(1)} %get-tuple-element.32), channel_id=1, source_target_pairs={{2,0},{4,2},{6,4},{8,6},{10,8},{12,10},{14,12},{16,14},{18,16},{20... | collective-permute-start | bytes 4616 | tf_op jit(solution)/shard_map/ppermute | solution.py:20
  12.1 5.9 %collective-permute-start = (bf16[3,256]{1,0:T(4,128)(2,1)S(1)}, bf16[3,256]{1,0:T(4,128)(2,1)S(1)}, u32[]{:S(2)}, u32[]{:S(2)}) collective-permute-start(bf16[3,256]{1,0:T(4,128)(2,1)S(1)} %get-tuple-element.33), channel_id=1, source_target_pairs={{0,2},{2,4},{4,6},{6,8},{8,10},{10,12},{12,14},{14,16},{16,18},{18... | collective-permute-start | bytes 4616 | tf_op jit(solution)/shard_map/ppermute | solution.py:18
  15.4 24.2 %copy-start.46 = (pred[512]{0:T(512)(128)(4,1)}, pred[512]{0:T(512)(128)(4,1)S(1)}, u32[]{:S(2)}) copy-start(pred[512]{0:T(512)(128)(4,1)S(1)} %get-tuple-element.47) | copy-start | bytes 1540
  15.4 29.1 %copy-start.49 = (pred[512]{0:T(512)(128)(4,1)}, pred[512]{0:T(512)(128)(4,1)S(1)}, u32[]{:S(2)}) copy-start(pred[512]{0:T(512)(128)(4,1)S(1)} %get-tuple-element.43) | copy-start | bytes 1540
  15.5 16.0 %copy-start.19 = (pred[512]{0:T(512)(128)(4,1)}, pred[512]{0:T(512)(128)(4,1)S(1)}, u32[]{:S(2)}) copy-start(pred[512]{0:T(512)(128)(4,1)S(1)} %get-tuple-element.40) | copy-start | bytes 1540
  15.5 16.1 %copy-start.35 = (pred[512]{0:T(512)(128)(4,1)}, pred[512]{0:T(512)(128)(4,1)S(1)}, u32[]{:S(2)}) copy-start(pred[512]{0:T(512)(128)(4,1)S(1)} %get-tuple-element.37) | copy-start | bytes 1540
  15.5 24.2 %copy-start.38 = (pred[512]{0:T(512)(128)(4,1)}, pred[512]{0:T(512)(128)(4,1)S(1)}, u32[]{:S(2)}) copy-start(pred[512]{0:T(512)(128)(4,1)S(1)} %get-tuple-element.35) | copy-start | bytes 1540
  15.5 24.3 %copy-start.23 = (pred[512]{0:T(512)(128)(4,1)}, pred[512]{0:T(512)(128)(4,1)S(1)}, u32[]{:S(2)}) copy-start(pred[512]{0:T(512)(128)(4,1)S(1)} %get-tuple-element.39) | copy-start | bytes 1540
  15.6 28.8 %copy-start.21 = (pred[512]{0:T(512)(128)(4,1)}, pred[512]{0:T(512)(128)(4,1)S(1)}, u32[]{:S(2)}) copy-start(pred[512]{0:T(512)(128)(4,1)S(1)} %get-tuple-element.36) | copy-start | bytes 1540
  15.6 29.1 %copy-start.41 = (pred[512]{0:T(512)(128)(4,1)}, pred[512]{0:T(512)(128)(4,1)S(1)}, u32[]{:S(2)}) copy-start(pred[512]{0:T(512)(128)(4,1)S(1)} %get-tuple-element.34) | copy-start | bytes 1540
  21.0 12.2 %copy-start.4 = (f32[512,256]{1,0:T(8,128)}, f32[512,256]{1,0:T(8,128)S(1)}, u32[]{:S(2)}) copy-start(f32[512,256]{1,0:T(8,128)S(1)} %get-tuple-element.52) | copy-start | bytes 1572868
  21.0 5.9 %collective-permute-start.2 = (bf16[9,256]{1,0:T(8,128)(2,1)S(1)}, bf16[9,256]{1,0:T(8,128)(2,1)S(1)}, u32[]{:S(2)}, u32[]{:S(2)}) collective-permute-start(bf16[9,256]{1,0:T(8,128)(2,1)S(1)} %get-tuple-element.31), channel_id=1, source_target_pairs={{0,2},{2,4},{4,6},{6,8},{8,10},{10,12},{12,14},{14,16},{16,18},{18... | collective-permute-start | bytes 13832 | tf_op jit(solution)/shard_map/ppermute | solution.py:18
  24.8 6.7 %collective-permute-start.3 = (bf16[9,256]{1,0:T(8,128)(2,1)S(1)}, bf16[9,256]{1,0:T(8,128)(2,1)S(1)}, u32[]{:S(2)}, u32[]{:S(2)}) collective-permute-start(bf16[9,256]{1,0:T(8,128)(2,1)S(1)} %get-tuple-element.30), channel_id=1, source_target_pairs={{2,0},{4,2},{6,4},{8,6},{10,8},{12,10},{14,12},{16,14},{18,16},{20... | collective-permute-start | bytes 13832 | tf_op jit(solution)/shard_map/ppermute | solution.py:20
  33.6 23.4 %copy-start.10 = (f32[512,256]{1,0:T(8,128)}, f32[512,256]{1,0:T(8,128)S(1)}, u32[]{:S(2)}) copy-start(f32[512,256]{1,0:T(8,128)S(1)} %get-tuple-element.54) | copy-start | bytes 1572868
  33.7 5.9 %collective-permute-start.4 = (bf16[27,256]{1,0:T(8,128)(2,1)S(1)}, bf16[27,256]{1,0:T(8,128)(2,1)S(1)}, u32[]{:S(2)}, u32[]{:S(2)}) collective-permute-start(bf16[27,256]{1,0:T(8,128)(2,1)S(1)} %get-tuple-element.29), channel_id=1, source_target_pairs={{0,2},{2,4},{4,6},{6,8},{8,10},{10,12},{12,14},{14,16},{16,18},{18... | collective-permute-start | bytes 41480 | tf_op jit(solution)/shard_map/ppermute | solution.py:18
  37.6 6.7 %collective-permute-start.5 = (bf16[27,256]{1,0:T(8,128)(2,1)S(1)}, bf16[27,256]{1,0:T(8,128)(2,1)S(1)}, u32[]{:S(2)}, u32[]{:S(2)}) collective-permute-start(bf16[27,256]{1,0:T(8,128)(2,1)S(1)} %get-tuple-element.28), channel_id=1, source_target_pairs={{2,0},{4,2},{6,4},{8,6},{10,8},{12,10},{14,12},{16,14},{18,16},{20... | collective-permute-start | bytes 41480 | tf_op jit(solution)/shard_map/ppermute | solution.py:20
  46.9 7.4 %collective-permute-start.6 = (bf16[27,256]{1,0:T(8,128)(2,1)}, bf16[27,256]{1,0:T(8,128)(2,1)S(1)}, u32[]{:S(2)}, u32[]{:S(2)}) collective-permute-start(bf16[27,256]{1,0:T(8,128)(2,1)} %get-tuple-element.27), channel_id=1, source_target_pairs={{2,0},{4,2},{6,4},{8,6},{10,8},{12,10},{14,12},{16,14},{18,16},{20... | collective-permute-start | bytes 41480 | tf_op jit(solution)/shard_map/ppermute | solution.py:20
  50.2 6.4 %collective-permute-start.7 = (bf16[27,256]{1,0:T(8,128)(2,1)}, bf16[27,256]{1,0:T(8,128)(2,1)S(1)}, u32[]{:S(2)}, u32[]{:S(2)}) collective-permute-start(bf16[27,256]{1,0:T(8,128)(2,1)} %get-tuple-element.26), channel_id=1, source_target_pairs={{0,2},{2,4},{4,6},{6,8},{8,10},{10,12},{12,14},{14,16},{16,18},{18... | collective-permute-start | bytes 41480 | tf_op jit(solution)/shard_map/ppermute | solution.py:18
  59.4 6.7 %collective-permute-start.8 = (bf16[9,256]{1,0:T(8,128)(2,1)S(1)}, bf16[9,256]{1,0:T(8,128)(2,1)S(1)}, u32[]{:S(2)}, u32[]{:S(2)}) collective-permute-start(bf16[9,256]{1,0:T(8,128)(2,1)S(1)} %get-tuple-element.25), channel_id=1, source_target_pairs={{2,0},{4,2},{6,4},{8,6},{10,8},{12,10},{14,12},{16,14},{18,16},{20... | collective-permute-start | bytes 13832 | tf_op jit(solution)/shard_map/ppermute | solution.py:20
  62.0 5.7 %collective-permute-start.9 = (bf16[9,256]{1,0:T(8,128)(2,1)S(1)}, bf16[9,256]{1,0:T(8,128)(2,1)S(1)}, u32[]{:S(2)}, u32[]{:S(2)}) collective-permute-start(bf16[9,256]{1,0:T(8,128)(2,1)S(1)} %get-tuple-element.24), channel_id=1, source_target_pairs={{0,2},{2,4},{4,6},{6,8},{8,10},{10,12},{12,14},{14,16},{16,18},{18... | collective-permute-start | bytes 13832 | tf_op jit(solution)/shard_map/ppermute | solution.py:18
  71.1 7.0 %collective-permute-start.10 = (bf16[3,256]{1,0:T(4,128)(2,1)}, bf16[3,256]{1,0:T(4,128)(2,1)}, u32[]{:S(2)}, u32[]{:S(2)}) collective-permute-start(bf16[3,256]{1,0:T(4,128)(2,1)} %get-tuple-element.23), channel_id=1, source_target_pairs={{2,0},{4,2},{6,4},{8,6},{10,8},{12,10},{14,12},{16,14},{18,16},{20... | collective-permute-start | bytes 4616 | tf_op jit(solution)/shard_map/ppermute | solution.py:20
  73.7 6.9 %collective-permute-start.11 = (bf16[3,256]{1,0:T(4,128)(2,1)}, bf16[3,256]{1,0:T(4,128)(2,1)S(1)}, u32[]{:S(2)}, u32[]{:S(2)}) collective-permute-start(bf16[3,256]{1,0:T(4,128)(2,1)} %get-tuple-element.22), channel_id=1, source_target_pairs={{0,2},{2,4},{4,6},{6,8},{8,10},{10,12},{12,14},{14,16},{16,18},{18... | collective-permute-start | bytes 4616 | tf_op jit(solution)/shard_map/ppermute | solution.py:18
  81.7 3.4 collective-permute-start.12
  86.7 14.6 %copy-start.42 = (pred[512]{0:T(512)(128)(4,1)S(1)}, pred[512]{0:T(512)(128)(4,1)}, u32[]{:S(2)}) copy-start(pred[512]{0:T(512)(128)(4,1)} %copy-done.41) | copy-start | bytes 1540
  89.0 12.4 %copy-start.50 = (pred[512]{0:T(512)(128)(4,1)S(1)}, pred[512]{0:T(512)(128)(4,1)}, u32[]{:S(2)}) copy-start(pred[512]{0:T(512)(128)(4,1)} %copy-done.49) | copy-start | bytes 1540
  89.0 12.7 %collective-permute-start.14 = (bf16[27,256]{1,0:T(8,128)(2,1)S(1)}, bf16[27,256]{1,0:T(8,128)(2,1)S(1)}, u32[]{:S(2)}, u32[]{:S(2)}) collective-permute-start(bf16[27,256]{1,0:T(8,128)(2,1)S(1)} %get-tuple-element.20), channel_id=1, source_target_pairs={{0,2},{2,4},{4,6},{6,8},{8,10},{10,12},{12,14},{14,16},{16,18},{18... | collective-permute-start | bytes 41480 | tf_op jit(solution)/shard_map/ppermute | solution.py:18
  94.1 7.1 %collective-permute-start.13 = (bf16[27,256]{1,0:T(8,128)(2,1)S(1)}, bf16[27,256]{1,0:T(8,128)(2,1)S(1)}, u32[]{:S(2)}, u32[]{:S(2)}) collective-permute-start(bf16[27,256]{1,0:T(8,128)(2,1)S(1)} %get-tuple-element.21), channel_id=1, source_target_pairs={{2,0},{4,2},{6,4},{8,6},{10,8},{12,10},{14,12},{16,14},{18,16},{20... | collective-permute-start | bytes 41480 | tf_op jit(solution)/shard_map/ppermute | solution.py:20
  105.2 6.6 %collective-permute-start.15 = (bf16[9,256]{1,0:T(8,128)(2,1)S(1)}, bf16[9,256]{1,0:T(8,128)(2,1)S(1)}, u32[]{:S(2)}, u32[]{:S(2)}) collective-permute-start(bf16[9,256]{1,0:T(8,128)(2,1)S(1)} %get-tuple-element.19), channel_id=1, source_target_pairs={{2,0},{4,2},{6,4},{8,6},{10,8},{12,10},{14,12},{16,14},{18,16},{20... | collective-permute-start | bytes 13832 | tf_op jit(solution)/shard_map/ppermute | solution.py:20
  107.6 5.6 %collective-permute-start.16 = (bf16[9,256]{1,0:T(8,128)(2,1)S(1)}, bf16[9,256]{1,0:T(8,128)(2,1)S(1)}, u32[]{:S(2)}, u32[]{:S(2)}) collective-permute-start(bf16[9,256]{1,0:T(8,128)(2,1)S(1)} %get-tuple-element.18), channel_id=1, source_target_pairs={{0,2},{2,4},{4,6},{6,8},{8,10},{10,12},{12,14},{14,16},{16,18},{18... | collective-permute-start | bytes 13832 | tf_op jit(solution)/shard_map/ppermute | solution.py:18
  117.1 7.5 %collective-permute-start.17 = (bf16[3,256]{1,0:T(4,128)(2,1)S(1)}, bf16[3,256]{1,0:T(4,128)(2,1)S(1)}, u32[]{:S(2)}, u32[]{:S(2)}) collective-permute-start(bf16[3,256]{1,0:T(4,128)(2,1)S(1)} %get-tuple-element.17), channel_id=1, source_target_pairs={{2,0},{4,2},{6,4},{8,6},{10,8},{12,10},{14,12},{16,14},{18,16},{20... | collective-permute-start | bytes 4616 | tf_op jit(solution)/shard_map/ppermute | solution.py:20
  119.4 8.6 %collective-permute-start.18 = (bf16[3,256]{1,0:T(4,128)(2,1)S(1)}, bf16[3,256]{1,0:T(4,128)(2,1)S(1)}, u32[]{:S(2)}, u32[]{:S(2)}) collective-permute-start(bf16[3,256]{1,0:T(4,128)(2,1)S(1)} %get-tuple-element.16), channel_id=1, source_target_pairs={{0,2},{2,4},{4,6},{6,8},{8,10},{10,12},{12,14},{14,16},{16,18},{18... | collective-permute-start | bytes 4616 | tf_op jit(solution)/shard_map/ppermute | solution.py:18
  (63 other events, 288.8 us)
Sparse Core Ops, SparseCore 0:
  130.9 245.2 all-reduce.2

commit v4 on v1

--- a/solution.py
+++ b/solution.py
@@ -46,46 +46,50 @@
 
 
 def shards(saved_input, upstream, clip_lengths, conv_a, bias_a, conv_b):
-    stream = saved_input[0, 0]
     lengths = clip_lengths[0]
     weights_a = conv_a[0]
     biases_a = bias_a[0]
     weights_b = conv_b[0]
-    frames = stream.shape[0]
-    channels = stream.shape[1]
+    frames = saved_input.shape[2]
+    channels = saved_input.shape[3]
     inner = weights_a.shape[3]
     half = KERNEL // 2
-    furthest = half * 3 ** (UNITS - 1)
+    reaches = [half * 3**unit_idx for unit_idx in range(UNITS)]
+    margin = 3 * sum(reaches)
+    span = frames + 2 * margin
+    total = frames * lax.axis_size("seq")
     offset = lax.axis_index("seq") * frames
     is_decoder = lax.axis_index("segment") == 1
     clip_ends = jnp.cumsum(lengths)
-    places = offset - furthest + jnp.arange(frames + 2 * furthest, dtype=jnp.int32)
+    places = offset - margin + jnp.arange(span, dtype=jnp.int32)
     clip_of = jnp.sum((places[:, None] >= clip_ends[None, :]).astype(jnp.int32), axis=1)
-    own_clip = clip_of[furthest : furthest + frames]
+    clip_of = jnp.where(places < 0, -1, clip_of)
+    clip_of = jnp.where(places >= total, lengths.shape[0], clip_of)
+    own = slice(margin, margin + frames)
 
     def linked(shift_by):
-        return (clip_of[furthest + shift_by : furthest + shift_by + frames] == own_clip)[:, None]
+        edge = abs(shift_by)
+        padded_ids = jnp.pad(clip_of, (edge, edge), constant_values=-2)
+        return (padded_ids[edge + shift_by : edge + shift_by + span] == clip_of)[:, None]
+
+    def shifted_rows(values, shift_by):
+        edge = abs(shift_by)
+        padded = jnp.pad(values, ((edge, edge), (0, 0)))
+        return jnp.where(
+            linked(shift_by),
+            padded[edge + shift_by : edge + shift_by + span],
+            jnp.zeros((), values.dtype),
+        )
+
+    stream = with_halo(saved_input[0, 0], (("seq", 0),), margin)
+    grad_top = with_halo(upstream[0], (("seq", 0),), margin)
 
     stored = []
     for unit_idx in range(UNITS):
         dilation = 3**unit_idx
-        reach = half * dilation
         active = elu_act(stream.astype(jnp.float32)).astype(jnp.bfloat16)
-        padded = spread_acts(active, reach)
         tap_rows = jnp.concatenate(
-            [
-                jnp.where(
-                    linked((tap_no - half) * dilation),
-                    padded[
-                        reach
-                        + (tap_no - half) * dilation : reach
-                        + (tap_no - half) * dilation
-                        + frames
-                    ],
-                    jnp.zeros((), jnp.bfloat16),
-                )
-                for tap_no in range(KERNEL)
-            ],
+            [shifted_rows(active, (tap_no - half) * dilation) for tap_no in range(KERNEL)],
             axis=1,
         )
         pre_act = biases_a[unit_idx][None, :] + jnp.dot(
@@ -103,7 +107,6 @@
 
     def unit_back(unit_idx, grad_y):
         dilation = 3**unit_idx
-        reach = half * dilation
         stream_in, tap_rows, pre_act, squashed = stored[unit_idx]
         grad_b = lax.dot_general(
             grad_y,
@@ -112,21 +115,8 @@
             preferred_element_type=jnp.float32,
         )
         gate = (grad_b * elu_slope(pre_act)).astype(jnp.bfloat16)
-        gate_padded = spread_grads(gate, reach)
         back_rows = jnp.concatenate(
-            [
-                jnp.where(
-                    linked(-(tap_no - half) * dilation),
-                    gate_padded[
-                        reach
-                        - (tap_no - half) * dilation : reach
-                        - (tap_no - half) * dilation
-                        + frames
-                    ],
-                    jnp.zeros((), jnp.bfloat16),
-                )
-                for tap_no in range(KERNEL)
-            ],
+            [shifted_rows(gate, -(tap_no - half) * dilation) for tap_no in range(KERNEL)],
             axis=1,
         )
         turned = jnp.transpose(weights_a[unit_idx], (0, 2, 1)).reshape(KERNEL * inner, channels)
@@ -138,7 +128,7 @@
 
     first_gates = [None] * UNITS
     first_grads = [None] * (UNITS + 1)
-    grad_y = upstream[0]
+    grad_y = grad_top
     first_grads[UNITS] = grad_y
     for unit_idx in reversed(range(UNITS)):
         gate, grad_y = unit_back(unit_idx, grad_y)
@@ -153,18 +143,20 @@
     for unit_idx in reversed(range(UNITS)):
         stream_in, tap_rows, pre_act, squashed = stored[unit_idx]
         gate_two, grad_next = unit_back(unit_idx, grad_y)
-        gate = jnp.where(is_decoder, first_gates[unit_idx], gate_two)
-        grad_out = jnp.where(is_decoder, first_grads[unit_idx + 1], grad_y)
-        unit_b = lax.dot_general(squashed, grad_out, contract, preferred_element_type=jnp.float32)
+        gate = jnp.where(is_decoder, first_gates[unit_idx][own], gate_two[own])
+        grad_out = jnp.where(is_decoder, first_grads[unit_idx + 1][own], grad_y[own])
+        unit_b = lax.dot_general(
+            squashed[own], grad_out, contract, preferred_element_type=jnp.float32
+        )
         unit_bias = jnp.sum(gate.astype(jnp.float32), axis=0)
         unit_a = lax.dot_general(
-            tap_rows, gate, contract, preferred_element_type=jnp.float32
+            tap_rows[own], gate, contract, preferred_element_type=jnp.float32
         ).reshape(KERNEL, channels, inner)
         grads_a[unit_idx] = unit_a
         grads_bias[unit_idx] = unit_bias
         grads_b[unit_idx] = unit_b
         grad_y = grad_next
-    section_grad = jnp.where(is_decoder, first_grads[0], grad_y)
+    section_grad = jnp.where(is_decoder, first_grads[0][own], grad_y[own])
     rows_a = UNITS * KERNEL * channels
     rows_b = UNITS * inner
     packed = jnp.concatenate(

time: 398 us -> 342 us (0.86)
  starting transfers between devices: 57.5 us -> 13.6 us
  waiting for transfers between devices: 264 us -> 247 us
    ppermute x9 -> x2, starting transfers between devices: 37.1 us -> 7.64 us  [with_halo(): lax.ppermute(tail, axis, [(i, (i + 1) % count) for i in range(ends)])]
    ppermute x9 -> x2, starting transfers between devices: 19.2 us -> 4.64 us  [with_halo(): lax.ppermute(head, axis, [((i + 1) % count, i) for i in range(ends)])]
    ppermute x9 -> x2, waiting for transfers between devices: 13.2 us -> 0.01 us  [with_halo(): lax.ppermute(head, axis, [((i + 1) % count, i) for i in range(ends)])]
    unnamed x46 -> x47, other arithmetic: 10.3 us -> 8.7 us
  transfers between devices with their start and end apart: 20 -> 6, of which waited for: 8 -> 2; matrix products, arithmetic and copies ran while one was open for 5% -> 7% of each run, Pallas kernels for 0% -> 0%
where the time goes in v4:
time: 342 us; the launch traced here: 339 us
  waiting for transfers between devices  247 us (72%)
  local copies, waits for them, and re-layouts  26 us (8%)
  matrix products  19 us (6%)
  other arithmetic  17.8 us (5%)
  between operations  15.2 us (4%)
  starting transfers between devices  13.6 us (4%)
    psum x1, waiting for transfers between devices, shards(): packed = lax.psum(packed, ('dp', 'seq'))  245 us
    unnamed x47, other arithmetic  8.7 us
    transpose x4, local copies, waits for them, and re-layouts, unit_back(): jnp.transpose(weights_a[unit_idx], (0, 2, 1))  7.76 us
    ppermute x2, starting transfers between devices, with_halo(): lax.ppermute(tail, axis, [(i, (i + 1) % count) for i in range(ends)])  7.64 us
    dot_general x6, matrix products, unit_back(): back = jnp.dot(back_rows, turned, preferred_element_type=jnp.float32)  7.2 us
  transfers between devices with their start and end apart: 6, of which 2 were waited for; matrix products, arithmetic and copies ran while one was open for 7% of the time, Pallas kernels for 0%

profile of v4, /device:TPU:32, one launch (start us, length us, event | category | flops | bytes accessed | tf_op | source)
XLA Modules:
  0.0 339.0 jit_solution(5440736164505156868)
XLA Ops:
  7.2 0.9 slice_bitcast_fusion.1
  8.1 3.8 %collective-permute-start.2 = (bf16[117,256]{1,0:T(8,128)(2,1)S(1)}, bf16[117,256]{1,0:T(8,128)(2,1)S(1)}, u32[]{:S(2)}, u32[]{:S(2)}) collective-permute-start(bf16[117,256]{1,0:T(8,128)(2,1)S(1)} %get-tuple-element.14), channel_id=1, source_target_pairs={{0,2},{2,4},{4,6},{6,8},{8,10},{10,12},{12,14},{14,16},{16,18},{18... | collective-permute-start | bytes 179720 | tf_op jit(solution)/shard_map/ppermute | solution.py:18
  11.9 2.0 collective-permute-start.3
  13.9 1.5 slice_bitcast_fusion.3
  15.5 3.8 %collective-permute-start = (bf16[117,256]{1,0:T(8,128)(2,1)}, bf16[117,256]{1,0:T(8,128)(2,1)}, u32[]{:S(2)}, u32[]{:S(2)}) collective-permute-start(bf16[117,256]{1,0:T(8,128)(2,1)} %get-tuple-element.12), channel_id=1, source_target_pairs={{0,2},{2,4},{4,6},{6,8},{8,10},{10,12},{12,14},{14,16},{16,18},{18... | collective-permute-start | bytes 179720 | tf_op jit(solution)/shard_map/ppermute | solution.py:18
  19.3 2.6 collective-permute-start.1
  23.7 3.7 %slice_bitcast_fusion.6 = (bf16[7,256,256]{1,2,0:T(8,128)(2,1)S(1)}, bf16[7,256,256]{1,2,0:T(8,128)(2,1)S(1)}, bf16[7,256,256]{1,2,0:T(8,128)(2,1)S(1)}, bf16[1,...) fusion(bf16[1,3,7,256,256]{4,3,2,1,0:T(8,128)(2,1)} %param.9), kind=kLoop, calls=%fused_computation.203 | loop fusion | bytes 8257536 | tf_op jit(solution)/shard_map/transpose | solution.py:122
  27.9 1.4 copy.22
  29.3 1.4 copy.21
  30.6 1.4 copy.20
  34.0 1.0 fusion.25
  37.7 1.0 fusion.26
  41.2 0.9 broadcast_compare_fusion
  42.5 1.3 fusion.8
  45.0 1.8 add_convert_fusion.2
  48.3 1.0 fusion.15
  50.9 1.7 fusion.14
  52.7 1.3 collective-permute-start.4
  54.0 2.4 collective-permute-done.4
  56.5 1.5 fusion.11
  58.2 0.8 fusion
  60.4 0.9 add_convert_fusion.1
  63.4 0.8 fusion.2
  65.7 1.0 add_convert_fusion
  67.6 1.1 copy-done.17
  68.7 0.8 fusion.4
  71.4 3.1 pad_maximum_fusion
  75.7 0.9 fusion.62
  76.6 1.9 fusion.34
  78.5 244.9 %all-reduce.37.cloned.1.call-done = f32[6152,256]{1,0:T(8,128)} async-done(((f32[6152,256]{1,0:T(8,128)}), f32[6152,256]{1,0:T(8,128)}) %all-reduce.37.cloned.1.call-update) | async-done | bytes 6299664 | tf_op jit(solution)/shard_map/psum | solution.py:170
  324.7 2.1 slice.513
  326.8 5.4 %slice.511 = f32[5376,256]{1,0:T(8,128)} slice(f32[6152,256]{1,0:T(8,128)} %all-reduce.37.cloned.1.call-done), slice={[0:5376], [0:256]} | slice | bytes 11010048 | tf_op jit(solution)/shard_map/slice | solution.py:171
  (190 shorter events, 23.8 us)
Async XLA Ops:
  7.2 316.3 %all-reduce.37.cloned.1.call-start = ((), (), s32[]{:S(2)}) async-start(), calls=%async_computation | async-start | bytes 12599296 | tf_op jit(solution)/shard_map/psum | solution.py:170
  8.1 23.9 %collective-permute-start.2 = (bf16[117,256]{1,0:T(8,128)(2,1)S(1)}, bf16[117,256]{1,0:T(8,128)(2,1)S(1)}, u32[]{:S(2)}, u32[]{:S(2)}) collective-permute-start(bf16[117,256]{1,0:T(8,128)(2,1)S(1)} %get-tuple-element.14), channel_id=1, source_target_pairs={{0,2},{2,4},{4,6},{6,8},{8,10},{10,12},{12,14},{14,16},{16,18},{18... | collective-permute-start | bytes 179720 | tf_op jit(solution)/shard_map/ppermute | solution.py:18
  11.9 20.1 %collective-permute-start.3 = (bf16[117,256]{1,0:T(8,128)(2,1)S(1)}, bf16[117,256]{1,0:T(8,128)(2,1)S(1)}, u32[]{:S(2)}, u32[]{:S(2)}) collective-permute-start(bf16[117,256]{1,0:T(8,128)(2,1)S(1)} %get-tuple-element.15), channel_id=1, source_target_pairs={{2,0},{4,2},{6,4},{8,6},{10,8},{12,10},{14,12},{16,14},{18,16},{20... | collective-permute-start | bytes 179720 | tf_op jit(solution)/shard_map/ppermute | solution.py:20
  15.5 27.0 %collective-permute-start = (bf16[117,256]{1,0:T(8,128)(2,1)}, bf16[117,256]{1,0:T(8,128)(2,1)}, u32[]{:S(2)}, u32[]{:S(2)}) collective-permute-start(bf16[117,256]{1,0:T(8,128)(2,1)} %get-tuple-element.12), channel_id=1, source_target_pairs={{0,2},{2,4},{4,6},{6,8},{8,10},{10,12},{12,14},{14,16},{16,18},{18... | collective-permute-start | bytes 179720 | tf_op jit(solution)/shard_map/ppermute | solution.py:18
  19.3 23.2 %collective-permute-start.1 = (bf16[117,256]{1,0:T(8,128)(2,1)}, bf16[117,256]{1,0:T(8,128)(2,1)}, u32[]{:S(2)}, u32[]{:S(2)}) collective-permute-start(bf16[117,256]{1,0:T(8,128)(2,1)} %get-tuple-element.13), channel_id=1, source_target_pairs={{2,0},{4,2},{6,4},{8,6},{10,8},{12,10},{14,12},{16,14},{18,16},{20... | collective-permute-start | bytes 179720 | tf_op jit(solution)/shard_map/ppermute | solution.py:20
  23.7 3.7 %copy-start.30 = (f32[1,3,256]{2,0,1:T(1,128)S(1)}, f32[1,3,256]{2,0,1:T(1,128)}, u32[]{:S(2)}) copy-start(f32[1,3,256]{2,0,1:T(1,128)} %param.10) | copy-start | bytes 9220
  27.9 4.1 %copy-start = (bf16[1,1,512,256]{3,2,1,0:T(8,128)(2,1)S(1)}, bf16[1,1,512,256]{3,2,1,0:T(8,128)(2,1)}, u32[]{:S(2)}) copy-start(bf16[1,1,512,256]{3,2,1,0:T(8,128)(2,1)} %param.6) | copy-start | bytes 786436
  32.4 1.5 copy-start.9
  32.4 1.5 copy-start.33
  33.9 1.5 copy-start.16
  33.9 1.5 copy-start.22
  35.4 13.8 %copy-start.36 = (f32[746,256]{1,0:T(8,128)}, f32[746,256]{1,0:T(8,128)S(1)}, u32[]{:S(2)}) copy-start(f32[746,256]{1,0:T(8,128)S(1)} %get-tuple-element.34) | copy-start | bytes 2291716
  35.5 1.8 copy-start.25
  36.2 1.5 copy-start.8
  36.2 1.5 copy-start.32
  37.6 1.5 copy-start.18
  37.7 2.1 copy-start.26
  39.2 7.6 %copy-start.38 = (f32[746,256]{1,0:T(8,128)}, f32[746,256]{1,0:T(8,128)S(1)}, u32[]{:S(2)}) copy-start(f32[746,256]{1,0:T(8,128)S(1)} %get-tuple-element.38) | copy-start | bytes 2291716
  39.7 5.2 %copy-start.10 = (f32[746,256]{1,0:T(8,128)}, f32[746,256]{1,0:T(8,128)S(1)}, u32[]{:S(2)}) copy-start(f32[746,256]{1,0:T(8,128)S(1)} %get-tuple-element.40) | copy-start | bytes 2291716
  39.7 1.4 copy-start.7
  39.7 1.4 copy-start.31
  40.9 1.5 copy-start.20
  42.4 2.5 copy-start.44
  46.8 1.5 copy-start.42
  49.3 1.7 copy-start.40
  52.7 3.8 %collective-permute-start.4 = (bf16[746,256]{1,0:T(8,128)(2,1)}, bf16[746,256]{1,0:T(8,128)(2,1)S(1)}, u32[]{:S(2)}, u32[]{:S(2)}) collective-permute-start(bf16[746,256]{1,0:T(8,128)(2,1)} %fusion.14), channel_id=1, source_target_pairs={{1,0},{3,2},{5,4},{7,6},{9,8},{11,10},{13,12},{15,14},{17,16},{19,... | collective-permute-start | bytes 1145864 | tf_op jit(solution)/shard_map/ppermute | solution.py:137
  54.0 4.2 %copy-start.21 = (bf16[746,1792]{1,0:T(8,128)(2,1)S(1)}, bf16[746,1792]{1,0:T(8,128)(2,1)}, u32[]{:S(2)}) copy-start(bf16[746,1792]{1,0:T(8,128)(2,1)} %copy-done.20) | copy-start | bytes 8020996
  56.5 3.5 %copy-start.34 = (bf16[746,256]{1,0:T(8,128)(2,1)}, bf16[746,256]{1,0:T(8,128)(2,1)S(1)}, u32[]{:S(2)}) copy-start(bf16[746,256]{1,0:T(8,128)(2,1)S(1)} %collective-permute-done.4) | copy-start | bytes 1145860
  60.4 1.5 copy-start.39
  61.5 1.9 copy-start.19
  65.7 1.5 copy-start.37
  66.8 1.8 copy-start.17
  (22 other events, 24.5 us)
Sparse Core Ops, SparseCore 0:
  74.6 248.7 all-reduce.36

commit v5 on v4

--- a/solution.py
+++ b/solution.py
@@ -81,8 +81,11 @@
             jnp.zeros((), values.dtype),
         )
 
-    stream = with_halo(saved_input[0, 0], (("seq", 0),), margin)
-    grad_top = with_halo(upstream[0], (("seq", 0),), margin)
+    both = with_halo(
+        jnp.concatenate([saved_input[0, 0], upstream[0]], axis=1), (("seq", 0),), margin
+    )
+    stream = both[:, :channels]
+    grad_top = both[:, channels:]
 
     stored = []
     for unit_idx in range(UNITS):
@@ -159,18 +162,18 @@
     section_grad = jnp.where(is_decoder, first_grads[0][own], grad_y[own])
     rows_a = UNITS * KERNEL * channels
     rows_b = UNITS * inner
-    packed = jnp.concatenate(
+    flat_a = jnp.stack(grads_a).reshape(rows_a, inner)
+    flat_b = jnp.concatenate(
         [
-            jnp.stack(grads_a).reshape(rows_a, inner),
             jnp.stack(grads_b).reshape(rows_b, channels),
             jnp.pad(jnp.stack(grads_bias), ((0, 8 - UNITS), (0, 0))),
         ],
         axis=0,
     )
-    packed = lax.psum(packed, ("dp", "seq"))
-    total_a = packed[:rows_a].reshape(UNITS, KERNEL, channels, inner)
-    total_b = packed[rows_a : rows_a + rows_b].reshape(UNITS, inner, channels)
-    total_bias = packed[rows_a + rows_b : rows_a + rows_b + UNITS]
+    flat_a, flat_b = lax.psum((flat_a, flat_b), ("dp", "seq"))
+    total_a = flat_a.reshape(UNITS, KERNEL, channels, inner)
+    total_b = flat_b[:rows_b].reshape(UNITS, inner, channels)
+    total_bias = flat_b[rows_b : rows_b + UNITS]
     return (section_grad[None, None], total_a[None], total_bias[None], total_b[None])
 
 

time: 342 us -> 333 us (0.974)
  starting transfers between devices: 13.6 us -> 7.15 us
  other arithmetic: 17.8 us -> 21.6 us
  local copies, waits for them, and re-layouts: 26 us -> 22.2 us
    slice x5 -> x2, local copies, waits for them, and re-layouts: 10.5 us -> 2.76 us  [the longest x1 2.06 us: shards(): total_b = flat_b[:rows_b].reshape(UNITS, inner, channels)]
    ppermute x2 -> x1, starting transfers between devices: 7.64 us -> 2.12 us  [with_halo(): lax.ppermute(tail, axis, [(i, (i + 1) % count) for i in range(ends)])]
    unnamed x103 -> x92, local copies, waits for them, and re-layouts: 5.79 us -> 10.4 us
  transfers between devices with their start and end apart: 6 -> 4, of which waited for: 2 -> 2; matrix products, arithmetic and copies ran while one was open for 7% -> 4% of each run, Pallas kernels for 0% -> 0%
where the time goes in v5:
time: 333 us; the launch traced here: 331 us
  waiting for transfers between devices  245 us (74%)
  local copies, waits for them, and re-layouts  22.2 us (7%)
  other arithmetic  21.6 us (6%)
  matrix products  19.4 us (6%)
  between operations  15.2 us (5%)
  starting transfers between devices  7.15 us (2%)
    psum x1, waiting for transfers between devices, shards(): flat_a, flat_b = lax.psum((flat_a, flat_b), ('dp', 'seq'))  244 us
    unnamed x92, local copies, waits for them, and re-layouts  10.4 us
    unnamed x47, other arithmetic  8.64 us
    transpose x4, local copies, waits for them, and re-layouts, unit_back(): jnp.transpose(weights_a[unit_idx], (0, 2, 1))  7.72 us
    dot_general x6, matrix products, unit_back(): back = jnp.dot(back_rows, turned, preferred_element_type=jnp.float32)  7.42 us
  transfers between devices with their start and end apart: 4, of which 2 were waited for; matrix products, arithmetic and copies ran while one was open for 4% of the time, Pallas kernels for 0%

profile of v5, /device:TPU:32, one launch (start us, length us, event | category | flops | bytes accessed | tf_op | source)
XLA Modules:
  0.0 330.9 jit_solution(6688964839273164889)
XLA Ops:
  7.2 1.6 pad_maximum_fusion.4
  8.8 3.7 %collective-permute-start.1 = (bf16[117,512]{1,0:T(8,128)(2,1)}, bf16[117,512]{1,0:T(8,128)(2,1)S(1)}, u32[]{:S(2)}, u32[]{:S(2)}) collective-permute-start(bf16[117,512]{1,0:T(8,128)(2,1)} %get-tuple-element.15), channel_id=1, source_target_pairs={{2,0},{4,2},{6,4},{8,6},{10,8},{12,10},{14,12},{16,14},{18,16},{20... | collective-permute-start | bytes 359432 | tf_op jit(solution)/shard_map/ppermute | solution.py:20
  12.5 2.1 collective-permute-start
  16.4 3.5 %slice_bitcast_fusion.2 = (bf16[7,256,256]{1,2,0:T(8,128)(2,1)S(1)}, bf16[7,256,256]{1,2,0:T(8,128)(2,1)S(1)}, bf16[7,256,256]{1,2,0:T(8,128)(2,1)S(1)}, bf16[1,...) fusion(bf16[1,3,7,256,256]{4,3,2,1,0:T(8,128)(2,1)} %param.9), kind=kLoop, calls=%fused_computation.200 | loop fusion | bytes 8257536 | tf_op jit(solution)/shard_map/transpose | solution.py:125
  19.9 1.4 copy.20
  21.3 1.4 copy.21
  22.7 1.4 copy.22
  24.1 1.1 pad_maximum_fusion.2
  27.0 1.0 fusion.25
  30.7 1.0 fusion.26
  34.3 0.9 broadcast_compare_fusion
  37.1 0.9 add_convert_fusion.2
  39.6 1.0 fusion.15
  42.2 1.7 fusion.14
  43.9 1.3 collective-permute-start.2
  45.2 1.2 broadcast_minimum_fusion
  46.4 1.5 collective-permute-done.2
  47.8 1.7 fusion.11
  50.9 2.0 add_convert_fusion.1
  53.5 0.8 fusion
  54.3 0.9 copy-done.20
  55.3 0.8 fusion.2
  57.4 1.0 add_convert_fusion
  59.3 0.8 fusion.4
  61.7 1.5 convolution_bitcast_fusion
  63.3 1.0 pad_maximum_fusion
  64.3 2.8 maximum_bitcast_fusion
  68.3 0.9 fusion.62
  69.3 1.9 fusion.35
  71.2 243.9 %all-reduce.38.cloned.1.call-done = (f32[1,3,7,256,256]{4,3,2,1,0:T(8,128)}, f32[776,256]{1,0:T(8,128)}) async-done(((f32[1,3,7,256,256]{4,3,2,1,0:T(8,128)}, f32[776,256]{1,0:T(8,128)}), (f32[1,3,7,256,256]{4,3,2,1,0:T(8,128)}, f32[776,256]{1,0:T(8,128)})) %all-reduce.38.cloned.1.call-update) | async-done | bytes 6299664 | tf_op jit(solution)/shard_map/psum | solution.py:173
  315.8 2.1 slice.497
  318.5 5.6 %copy.79 = f32[1,3,7,256,256]{4,3,2,1,0:T(8,128)} copy(f32[1,3,7,256,256]{4,3,2,1,0:T(8,128)} %get-tuple-element.46) | data formatting | bytes 11010048
  (174 shorter events, 21.5 us)
Async XLA Ops:
  7.2 308.0 %all-reduce.38.cloned.1.call-start = ((), (), s32[]{:S(2)}) async-start(), calls=%async_computation | async-start | bytes 12599296 | tf_op jit(solution)/shard_map/psum | solution.py:173
  8.8 15.3 %collective-permute-start.1 = (bf16[117,512]{1,0:T(8,128)(2,1)}, bf16[117,512]{1,0:T(8,128)(2,1)S(1)}, u32[]{:S(2)}, u32[]{:S(2)}) collective-permute-start(bf16[117,512]{1,0:T(8,128)(2,1)} %get-tuple-element.15), channel_id=1, source_target_pairs={{2,0},{4,2},{6,4},{8,6},{10,8},{12,10},{14,12},{16,14},{18,16},{20... | collective-permute-start | bytes 359432 | tf_op jit(solution)/shard_map/ppermute | solution.py:20
  12.5 11.6 %collective-permute-start = (bf16[117,512]{1,0:T(8,128)(2,1)S(1)}, bf16[117,512]{1,0:T(8,128)(2,1)}, u32[]{:S(2)}, u32[]{:S(2)}) collective-permute-start(bf16[117,512]{1,0:T(8,128)(2,1)S(1)} %get-tuple-element.14), channel_id=1, source_target_pairs={{0,2},{2,4},{4,6},{6,8},{8,10},{10,12},{12,14},{14,16},{16,18},{18... | collective-permute-start | bytes 359432 | tf_op jit(solution)/shard_map/ppermute | solution.py:18
  19.9 4.2 %copy-start = (bf16[1,1,512,256]{3,2,1,0:T(8,128)(2,1)S(1)}, bf16[1,1,512,256]{3,2,1,0:T(8,128)(2,1)}, u32[]{:S(2)}) copy-start(bf16[1,1,512,256]{3,2,1,0:T(8,128)(2,1)} %param.6) | copy-start | bytes 786436
  19.9 4.2 %copy-start.1 = (bf16[1,512,256]{2,1,0:T(8,128)(2,1)S(1)}, bf16[1,512,256]{2,1,0:T(8,128)(2,1)}, u32[]{:S(2)}) copy-start(bf16[1,512,256]{2,1,0:T(8,128)(2,1)} %param.7) | copy-start | bytes 786436
  21.3 2.8 copy-start.31
  25.5 1.4 copy-start.10
  27.0 1.6 copy-start.17
  27.0 1.5 copy-start.23
  28.5 12.0 %copy-start.32 = (f32[746,256]{1,0:T(8,128)}, f32[746,256]{1,0:T(8,128)S(1)}, u32[]{:S(2)}) copy-start(f32[746,256]{1,0:T(8,128)S(1)} %get-tuple-element.34) | copy-start | bytes 2291716
  28.5 1.8 copy-start.26
  29.3 1.5 copy-start.9
  30.7 1.6 copy-start.19
  30.7 2.1 copy-start.27
  32.3 5.7 %copy-start.34 = (f32[746,256]{1,0:T(8,128)}, f32[746,256]{1,0:T(8,128)S(1)}, u32[]{:S(2)}) copy-start(f32[746,256]{1,0:T(8,128)S(1)} %get-tuple-element.38) | copy-start | bytes 2291716
  32.3 1.3 copy-start.29
  32.8 4.3 %copy-start.13 = (f32[746,256]{1,0:T(8,128)}, f32[746,256]{1,0:T(8,128)S(1)}, u32[]{:S(2)}) copy-start(f32[746,256]{1,0:T(8,128)S(1)} %get-tuple-element.40) | copy-start | bytes 2291716
  32.9 1.4 copy-start.8
  34.0 1.5 copy-start.21
  35.6 2.5 copy-start.11
  38.0 1.5 copy-start.36
  40.5 1.7 copy-start.38
  40.9 1.3 copy-start.2
  43.9 3.9 %collective-permute-start.2 = (bf16[746,256]{1,0:T(8,128)(2,1)}, bf16[746,256]{1,0:T(8,128)(2,1)}, u32[]{:S(2)}, u32[]{:S(2)}) collective-permute-start(bf16[746,256]{1,0:T(8,128)(2,1)} %fusion.14), channel_id=1, source_target_pairs={{1,0},{3,2},{5,4},{7,6},{9,8},{11,10},{13,12},{15,14},{17,16},{19,... | collective-permute-start | bytes 1145864 | tf_op jit(solution)/shard_map/ppermute | solution.py:140
  49.5 1.4 copy-start.14
  50.9 2.0 copy-start.24
  50.9 2.1 copy-start.35
  50.9 2.6 copy-start.22
  53.5 1.8 copy-start.20
  57.3 2.0 copy-start.18
  58.5 2.3 copy-start.15
  60.3 1.4 copy-start.12
  (14 other events, 14.6 us)
Sparse Core Ops, SparseCore 0:
  67.3 247.8 all-reduce.37

commit v6 on v5

--- a/solution.py
+++ b/solution.py
@@ -55,7 +55,8 @@
     inner = weights_a.shape[3]
     half = KERNEL // 2
     reaches = [half * 3**unit_idx for unit_idx in range(UNITS)]
-    margin = 3 * sum(reaches)
+    margin = -(-3 * sum(reaches) // 8) * 8
+    window = -(-(sum(reaches) + 1) // 8) * 8
     span = frames + 2 * margin
     total = frames * lax.axis_size("seq")
     offset = lax.axis_index("seq") * frames
@@ -67,17 +68,19 @@
     clip_of = jnp.where(places >= total, lengths.shape[0], clip_of)
     own = slice(margin, margin + frames)
 
-    def linked(shift_by):
+    def linked(shift_by, ids):
         edge = abs(shift_by)
-        padded_ids = jnp.pad(clip_of, (edge, edge), constant_values=-2)
-        return (padded_ids[edge + shift_by : edge + shift_by + span] == clip_of)[:, None]
-
-    def shifted_rows(values, shift_by):
+        rows = ids.shape[0]
+        padded_ids = jnp.pad(ids, (edge, edge), constant_values=-2)
+        return (padded_ids[edge + shift_by : edge + shift_by + rows] == ids)[:, None]
+
+    def shifted_rows(values, shift_by, ids=clip_of):
         edge = abs(shift_by)
+        rows = values.shape[0]
         padded = jnp.pad(values, ((edge, edge), (0, 0)))
         return jnp.where(
-            linked(shift_by),
-            padded[edge + shift_by : edge + shift_by + span],
+            linked(shift_by, ids),
+            padded[edge + shift_by : edge + shift_by + rows],
             jnp.zeros((), values.dtype),
         )
 
@@ -108,9 +111,12 @@
         stored.append((stream, tap_rows, pre_act, squashed))
         stream = next_stream
 
-    def unit_back(unit_idx, grad_y):
+    def unit_back(unit_idx, grad_y, rows=slice(0, span)):
         dilation = 3**unit_idx
         stream_in, tap_rows, pre_act, squashed = stored[unit_idx]
+        stream_in = stream_in[rows]
+        pre_act = pre_act[rows]
+        ids = clip_of[rows]
         grad_b = lax.dot_general(
             grad_y,
             weights_b[unit_idx],
@@ -119,7 +125,7 @@
         )
         gate = (grad_b * elu_slope(pre_act)).astype(jnp.bfloat16)
         back_rows = jnp.concatenate(
-            [shifted_rows(gate, -(tap_no - half) * dilation) for tap_no in range(KERNEL)],
+            [shifted_rows(gate, -(tap_no - half) * dilation, ids) for tap_no in range(KERNEL)],
             axis=1,
         )
         turned = jnp.transpose(weights_a[unit_idx], (0, 2, 1)).reshape(KERNEL * inner, channels)
@@ -142,12 +148,14 @@
     grads_bias = [None] * UNITS
     grads_b = [None] * UNITS
     contract = (((0,), (0,)), ((), ()))
-    grad_y = latent
+    near = slice(margin - window, margin + frames + window)
+    inside = slice(window, window + frames)
+    grad_y = latent[near]
     for unit_idx in reversed(range(UNITS)):
         stream_in, tap_rows, pre_act, squashed = stored[unit_idx]
-        gate_two, grad_next = unit_back(unit_idx, grad_y)
-        gate = jnp.where(is_decoder, first_gates[unit_idx][own], gate_two[own])
-        grad_out = jnp.where(is_decoder, first_grads[unit_idx + 1][own], grad_y[own])
+        gate_two, grad_next = unit_back(unit_idx, grad_y, near)
+        gate = jnp.where(is_decoder, first_gates[unit_idx][own], gate_two[inside])
+        grad_out = jnp.where(is_decoder, first_grads[unit_idx + 1][own], grad_y[inside])
         unit_b = lax.dot_general(
             squashed[own], grad_out, contract, preferred_element_type=jnp.float32
         )
@@ -159,7 +167,7 @@
         grads_bias[unit_idx] = unit_bias
         grads_b[unit_idx] = unit_b
         grad_y = grad_next
-    section_grad = jnp.where(is_decoder, first_grads[0][own], grad_y[own])
+    section_grad = jnp.where(is_decoder, first_grads[0][own], grad_y[inside])
     rows_a = UNITS * KERNEL * channels
     rows_b = UNITS * inner
     flat_a = jnp.stack(grads_a).reshape(rows_a, inner)

time: 333 us -> 322 us (0.967)
  matrix products: 19.4 us -> 14 us
  local copies, waits for them, and re-layouts: 22.2 us -> 17.1 us
    unnamed x92 -> x31, local copies, waits for them, and re-layouts: 10.4 us -> 5.94 us
    unnamed x47 -> x48, other arithmetic: 8.64 us -> 8.57 us
where the time goes in v6:
time: 322 us; the launch traced here: 319 us
  waiting for transfers between devices  248 us (77%)
  other arithmetic  18.4 us (6%)
  local copies, waits for them, and re-layouts  17.1 us (5%)
  between operations  15 us (5%)
  matrix products  14 us (4%)
  starting transfers between devices  7.18 us (2%)
    psum x1, waiting for transfers between devices, shards(): flat_a, flat_b = lax.psum((flat_a, flat_b), ('dp', 'seq'))  246 us
    unnamed x48, other arithmetic  8.57 us
    transpose x4, local copies, waits for them, and re-layouts, unit_back(): jnp.transpose(weights_a[unit_idx], (0, 2, 1))  6.97 us
  transfers between devices with their start and end apart: 4, of which 2 were waited for; matrix products, arithmetic and copies ran while one was open for 4% of the time, Pallas kernels for 0%

profile of v6, /device:TPU:32, one launch (start us, length us, event | category | flops | bytes accessed | tf_op | source)
XLA Modules:
  0.0 319.5 jit_solution(8940965927787928447)
XLA Ops:
  7.2 0.9 pad_maximum_fusion.4
  8.2 3.8 %collective-permute-start = (bf16[120,512]{1,0:T(8,128)(2,1)S(1)}, bf16[120,512]{1,0:T(8,128)(2,1)S(1)}, u32[]{:S(2)}, u32[]{:S(2)}) collective-permute-start(bf16[120,512]{1,0:T(8,128)(2,1)S(1)} %get-tuple-element.12), channel_id=1, source_target_pairs={{0,2},{2,4},{4,6},{6,8},{8,10},{10,12},{12,14},{14,16},{16,18},{18... | collective-permute-start | bytes 368648 | tf_op jit(solution)/shard_map/ppermute | solution.py:18
  12.0 2.0 collective-permute-start.1
  14.0 0.7 copy.19
  15.1 0.6 slice_compare_fusion.27
  15.8 3.5 %slice_bitcast_fusion.2 = (bf16[7,256,256]{1,2,0:T(8,128)(2,1)S(1)}, bf16[7,256,256]{1,2,0:T(8,128)(2,1)S(1)}, bf16[7,256,256]{1,2,0:T(8,128)(2,1)S(1)}, bf16[1,...) fusion(bf16[1,3,7,256,256]{4,3,2,1,0:T(8,128)(2,1)} %param.9), kind=kLoop, calls=%fused_computation.230 | loop fusion | bytes 8257536 | tf_op jit(solution)/shard_map/transpose | solution.py:131
  19.3 1.4 copy.20
  20.7 1.4 copy.21
  22.1 0.6 copy.22
  22.8 1.0 pad_maximum_fusion.2
  25.6 1.0 fusion.25
  28.6 1.0 fusion.26
  31.6 0.9 broadcast_compare_fusion
  34.0 0.9 add_convert_fusion
  36.5 1.0 fusion.10
  39.1 1.0 fusion.29
  40.1 1.3 collective-permute-start.2
  41.5 2.1 collective-permute-done.2
  44.9 0.8 add_convert_fusion.2
  47.0 0.8 add_convert_fusion.1
  48.9 0.7 fusion.4
  49.6 0.7 fusion.2
  50.3 0.7 fusion
  51.5 1.0 pad_maximum_fusion
  52.5 2.8 maximum_bitcast_fusion
  56.3 0.7 fusion.74
  57.2 0.9 fusion.51
  58.1 245.7 %all-reduce.45.cloned.1.call-done = (f32[1,3,7,256,256]{4,3,2,1,0:T(8,128)}, f32[776,256]{1,0:T(8,128)}) async-done(((f32[1,3,7,256,256]{4,3,2,1,0:T(8,128)}, f32[776,256]{1,0:T(8,128)}), (f32[1,3,7,256,256]{4,3,2,1,0:T(8,128)}, f32[776,256]{1,0:T(8,128)})) %all-reduce.45.cloned.1.call-update) | async-done | bytes 6299664 | tf_op jit(solution)/shard_map/psum | solution.py:181
  303.7 2.1 slice.582
  305.8 0.7 slice.581
  306.5 0.6 broadcast_in_dim.451
  307.1 5.6 %copy.79 = f32[1,3,7,256,256]{4,3,2,1,0:T(8,128)} copy(f32[1,3,7,256,256]{4,3,2,1,0:T(8,128)} %get-tuple-element.58) | data formatting | bytes 11010048
  (117 shorter events, 15.6 us)
Async XLA Ops:
  7.2 296.6 %all-reduce.45.cloned.1.call-start = ((), (), s32[]{:S(2)}) async-start(), calls=%async_computation | async-start | bytes 12599296 | tf_op jit(solution)/shard_map/psum | solution.py:181
  8.2 14.6 %collective-permute-start = (bf16[120,512]{1,0:T(8,128)(2,1)S(1)}, bf16[120,512]{1,0:T(8,128)(2,1)S(1)}, u32[]{:S(2)}, u32[]{:S(2)}) collective-permute-start(bf16[120,512]{1,0:T(8,128)(2,1)S(1)} %get-tuple-element.12), channel_id=1, source_target_pairs={{0,2},{2,4},{4,6},{6,8},{8,10},{10,12},{12,14},{14,16},{16,18},{18... | collective-permute-start | bytes 368648 | tf_op jit(solution)/shard_map/ppermute | solution.py:18
  12.0 10.8 %collective-permute-start.1 = (bf16[120,512]{1,0:T(8,128)(2,1)S(1)}, bf16[120,512]{1,0:T(8,128)(2,1)}, u32[]{:S(2)}, u32[]{:S(2)}) collective-permute-start(bf16[120,512]{1,0:T(8,128)(2,1)S(1)} %get-tuple-element.13), channel_id=1, source_target_pairs={{2,0},{4,2},{6,4},{8,6},{10,8},{12,10},{14,12},{16,14},{18,16},{20... | collective-permute-start | bytes 368648 | tf_op jit(solution)/shard_map/ppermute | solution.py:20
  20.7 2.0 copy-start.10
  20.7 2.1 copy-start
  20.7 2.1 copy-start.1
  24.1 1.4 copy-start.6
  25.6 1.1 copy-start.11
  27.1 1.4 copy-start.5
  30.1 1.3 copy-start.9
  30.1 1.5 copy-start.4
  32.9 1.2 copy-start.3
  35.3 1.2 copy-start.2
  40.1 4.4 %copy-start.7 = (bf16[752,256]{1,0:T(8,128)(2,1)}, bf16[752,256]{1,0:T(8,128)(2,1)S(1)}, u32[]{:S(2)}) copy-start(bf16[752,256]{1,0:T(8,128)(2,1)S(1)} %fusion.29) | copy-start | bytes 1155076
  40.1 3.6 %collective-permute-start.2 = (bf16[752,256]{1,0:T(8,128)(2,1)S(1)}, bf16[752,256]{1,0:T(8,128)(2,1)S(1)}, u32[]{:S(2)}, u32[]{:S(2)}) collective-permute-start(bf16[752,256]{1,0:T(8,128)(2,1)S(1)} %fusion.29), channel_id=1, source_target_pairs={{1,0},{3,2},{5,4},{7,6},{9,8},{11,10},{13,12},{15,14},{17,16},{19,... | collective-permute-start | bytes 1155080 | tf_op jit(solution)/shard_map/ppermute | solution.py:146
  56.2 1.0 copy-start.8
Sparse Core Ops, SparseCore 0:
  55.4 248.2 all-reduce.44

commit v7 on v6

--- a/solution.py
+++ b/solution.py
@@ -57,6 +57,7 @@
     reaches = [half * 3**unit_idx for unit_idx in range(UNITS)]
     margin = -(-3 * sum(reaches) // 8) * 8
     window = -(-(sum(reaches) + 1) // 8) * 8
+    reach_back = -(-(2 * sum(reaches) + 1) // 8) * 8
     span = frames + 2 * margin
     total = frames * lax.axis_size("seq")
     offset = lax.axis_index("seq") * frames
@@ -137,25 +138,29 @@
 
     first_gates = [None] * UNITS
     first_grads = [None] * (UNITS + 1)
-    grad_y = grad_top
+    far = slice(margin - reach_back, margin + frames + reach_back)
+    mine = slice(reach_back, reach_back + frames)
+    grad_y = grad_top[far]
     first_grads[UNITS] = grad_y
     for unit_idx in reversed(range(UNITS)):
-        gate, grad_y = unit_back(unit_idx, grad_y)
+        gate, grad_y = unit_back(unit_idx, grad_y, far)
         first_gates[unit_idx] = gate
         first_grads[unit_idx] = grad_y
-    latent = lax.ppermute(grad_y, "segment", [(1, 0)])
+    latent = lax.ppermute(
+        grad_y[reach_back - window : reach_back + frames + window], "segment", [(1, 0)]
+    )
     grads_a = [None] * UNITS
     grads_bias = [None] * UNITS
     grads_b = [None] * UNITS
     contract = (((0,), (0,)), ((), ()))
     near = slice(margin - window, margin + frames + window)
     inside = slice(window, window + frames)
-    grad_y = latent[near]
+    grad_y = latent
     for unit_idx in reversed(range(UNITS)):
         stream_in, tap_rows, pre_act, squashed = stored[unit_idx]
         gate_two, grad_next = unit_back(unit_idx, grad_y, near)
-        gate = jnp.where(is_decoder, first_gates[unit_idx][own], gate_two[inside])
-        grad_out = jnp.where(is_decoder, first_grads[unit_idx + 1][own], grad_y[inside])
+        gate = jnp.where(is_decoder, first_gates[unit_idx][mine], gate_two[inside])
+        grad_out = jnp.where(is_decoder, first_grads[unit_idx + 1][mine], grad_y[inside])
         unit_b = lax.dot_general(
             squashed[own], grad_out, contract, preferred_element_type=jnp.float32
         )
@@ -167,7 +172,7 @@
         grads_bias[unit_idx] = unit_bias
         grads_b[unit_idx] = unit_b
         grad_y = grad_next
-    section_grad = jnp.where(is_decoder, first_grads[0][own], grad_y[inside])
+    section_grad = jnp.where(is_decoder, first_grads[0][mine], grad_y[inside])
     rows_a = UNITS * KERNEL * channels
     rows_b = UNITS * inner
     flat_a = jnp.stack(grads_a).reshape(rows_a, inner)

time: 322 us -> 332 us (1.031)
  local copies, waits for them, and re-layouts: 17.1 us -> 24.2 us
    unnamed x31 -> x105, local copies, waits for them, and re-layouts: 5.94 us -> 12.2 us
where the time goes in v7:
time: 332 us; the launch traced here: 330 us
  waiting for transfers between devices  248 us (75%)
  local copies, waits for them, and re-layouts  24.2 us (7%)
  other arithmetic  18.7 us (6%)
  matrix products  16.8 us (5%)
  between operations  15.4 us (5%)
  starting transfers between devices  7.18 us (2%)
    psum x1, waiting for transfers between devices, shards(): flat_a, flat_b = lax.psum((flat_a, flat_b), ('dp', 'seq'))  245 us
    unnamed x105, local copies, waits for them, and re-layouts  12.2 us
    unnamed x48, other arithmetic  8.2 us
    transpose x4, local copies, waits for them, and re-layouts, unit_back(): jnp.transpose(weights_a[unit_idx], (0, 2, 1))  7.73 us
  transfers between devices with their start and end apart: 4, of which 2 were waited for; matrix products, arithmetic and copies ran while one was open for 4% of the time, Pallas kernels for 0%

profile of v7, /device:TPU:32, one launch (start us, length us, event | category | flops | bytes accessed | tf_op | source)
XLA Modules:
  0.0 329.9 jit_solution(11710837874884227373)
XLA Ops:
  7.2 0.9 pad_maximum_fusion.4
  8.2 3.8 %collective-permute-start = (bf16[120,512]{1,0:T(8,128)(2,1)S(1)}, bf16[120,512]{1,0:T(8,128)(2,1)S(1)}, u32[]{:S(2)}, u32[]{:S(2)}) collective-permute-start(bf16[120,512]{1,0:T(8,128)(2,1)S(1)} %get-tuple-element.12), channel_id=1, source_target_pairs={{0,2},{2,4},{4,6},{6,8},{8,10},{10,12},{12,14},{14,16},{16,18},{18... | collective-permute-start | bytes 368648 | tf_op jit(solution)/shard_map/ppermute | solution.py:18
  12.0 2.0 collective-permute-start.1
  14.0 0.7 copy.19
  15.8 3.5 %slice_bitcast_fusion.2 = (bf16[7,256,256]{1,2,0:T(8,128)(2,1)S(1)}, bf16[7,256,256]{1,2,0:T(8,128)(2,1)S(1)}, bf16[7,256,256]{1,2,0:T(8,128)(2,1)S(1)}, bf16[1,...) fusion(bf16[1,3,7,256,256]{4,3,2,1,0:T(8,128)(2,1)} %param.9), kind=kLoop, calls=%fused_computation.243 | loop fusion | bytes 8257536 | tf_op jit(solution)/shard_map/transpose | solution.py:132
  20.0 1.4 copy.20
  21.5 1.4 copy.21
  22.9 1.4 copy.22
  24.3 1.0 pad_maximum_fusion.2
  27.1 1.0 fusion.22
  30.6 1.0 fusion.24
  34.3 0.9 convolution_add_fusion
  37.3 0.9 add_convert_fusion
  39.8 0.9 fusion.12
  42.2 0.9 fusion.14
  43.1 1.3 collective-permute-start.2
  44.6 2.2 collective-permute-done.2
  46.7 1.5 fusion.15
  49.4 1.8 add_convert_fusion.2
  52.8 0.8 add_convert_fusion.1
  56.7 1.1 copy-done.16
  58.5 1.1 copy-done.12
  59.5 0.7 fusion
  60.7 1.4 convolution_bitcast_fusion
  62.1 1.0 pad_maximum_fusion
  63.1 2.8 maximum_bitcast_fusion
  67.1 0.7 fusion.74
  67.8 0.9 fusion.50
  68.8 245.4 %all-reduce.52.cloned.1.call-done = (f32[1,3,7,256,256]{4,3,2,1,0:T(8,128)}, f32[776,256]{1,0:T(8,128)}) async-done(((f32[1,3,7,256,256]{4,3,2,1,0:T(8,128)}, f32[776,256]{1,0:T(8,128)}), (f32[1,3,7,256,256]{4,3,2,1,0:T(8,128)}, f32[776,256]{1,0:T(8,128)})) %all-reduce.52.cloned.1.call-update) | async-done | bytes 6299664 | tf_op jit(solution)/shard_map/psum | solution.py:186
  314.2 2.1 slice.660
  316.2 0.7 slice.659
  317.5 5.6 %copy.79 = f32[1,3,7,256,256]{4,3,2,1,0:T(8,128)} copy(f32[1,3,7,256,256]{4,3,2,1,0:T(8,128)} %get-tuple-element.70) | data formatting | bytes 11010048
  (193 shorter events, 21.9 us)
Async XLA Ops:
  7.2 307.0 %all-reduce.52.cloned.1.call-start = ((), (), s32[]{:S(2)}) async-start(), calls=%async_computation | async-start | bytes 12599296 | tf_op jit(solution)/shard_map/psum | solution.py:186
  8.2 16.1 %collective-permute-start = (bf16[120,512]{1,0:T(8,128)(2,1)S(1)}, bf16[120,512]{1,0:T(8,128)(2,1)S(1)}, u32[]{:S(2)}, u32[]{:S(2)}) collective-permute-start(bf16[120,512]{1,0:T(8,128)(2,1)S(1)} %get-tuple-element.12), channel_id=1, source_target_pairs={{0,2},{2,4},{4,6},{6,8},{8,10},{10,12},{12,14},{14,16},{16,18},{18... | collective-permute-start | bytes 368648 | tf_op jit(solution)/shard_map/ppermute | solution.py:18
  12.0 12.3 %collective-permute-start.1 = (bf16[120,512]{1,0:T(8,128)(2,1)S(1)}, bf16[120,512]{1,0:T(8,128)(2,1)}, u32[]{:S(2)}, u32[]{:S(2)}) collective-permute-start(bf16[120,512]{1,0:T(8,128)(2,1)S(1)} %get-tuple-element.13), channel_id=1, source_target_pairs={{2,0},{4,2},{6,4},{8,6},{10,8},{12,10},{14,12},{16,14},{18,16},{20... | collective-permute-start | bytes 368648 | tf_op jit(solution)/shard_map/ppermute | solution.py:20
  21.5 2.8 copy-start.32
  21.5 2.8 copy-start
  21.5 2.8 copy-start.1
  22.9 2.9 copy-start.31
  22.9 3.1 copy-start.30
  24.2 2.3 copy-start.29
  25.2 1.4 copy-start.28
  27.1 1.5 copy-start.13
  27.1 1.5 copy-start.33
  28.6 1.4 copy-start.45
  28.6 12.0 %copy-start.35 = (f32[752,256]{1,0:T(8,128)}, f32[752,256]{1,0:T(8,128)S(1)}, u32[]{:S(2)}) copy-start(f32[752,256]{1,0:T(8,128)S(1)} %get-tuple-element.60) | copy-start | bytes 2310148
  30.6 1.6 copy-start.15
  30.6 2.1 copy-start.25
  32.2 1.5 copy-start.47
  32.2 6.0 %copy-start.39 = (f32[752,256]{1,0:T(8,128)}, f32[752,256]{1,0:T(8,128)S(1)}, u32[]{:S(2)}) copy-start(f32[752,256]{1,0:T(8,128)S(1)} %get-tuple-element.64) | copy-start | bytes 2310148
  32.9 1.3 copy-start.8
  34.2 1.5 copy-start.11
  34.2 1.8 copy-start.21
  35.7 2.4 copy-start.37
  38.1 1.6 copy-start.41
  40.6 1.6 copy-start.43
  43.1 3.6 %collective-permute-start.2 = (bf16[592,256]{1,0:T(8,128)(2,1)S(1)}, bf16[592,256]{1,0:T(8,128)(2,1)}, u32[]{:S(2)}, u32[]{:S(2)}) collective-permute-start(bf16[592,256]{1,0:T(8,128)(2,1)S(1)} %slice.632), channel_id=1, source_target_pairs={{1,0},{3,2},{5,4},{7,6},{9,8},{11,10},{13,12},{15,14},{17,16},{19,... | collective-permute-start | bytes 909320 | tf_op jit(solution)/shard_map/ppermute | solution.py:149
  49.4 1.9 copy-start.34
  49.4 1.9 copy-start.40
  52.8 1.4 copy-start.44
  52.8 1.4 copy-start.46
  54.2 1.8 copy-start.14
  56.0 1.8 copy-start.16
  57.8 1.8 copy-start.12
  (21 other events, 22.7 us)
Sparse Core Ops, SparseCore 0:
  66.1 248.0 all-reduce.51

commit v8 on v6

--- a/solution.py
+++ b/solution.py
@@ -124,12 +124,15 @@
             preferred_element_type=jnp.float32,
         )
         gate = (grad_b * elu_slope(pre_act)).astype(jnp.bfloat16)
-        back_rows = jnp.concatenate(
-            [shifted_rows(gate, -(tap_no - half) * dilation, ids) for tap_no in range(KERNEL)],
-            axis=1,
-        )
-        turned = jnp.transpose(weights_a[unit_idx], (0, 2, 1)).reshape(KERNEL * inner, channels)
-        back = jnp.dot(back_rows, turned, preferred_element_type=jnp.float32)
+        back = sum(
+            lax.dot_general(
+                shifted_rows(gate, -(tap_no - half) * dilation, ids),
+                weights_a[unit_idx, tap_no],
+                (((1,), (1,)), ((), ())),
+                preferred_element_type=jnp.float32,
+            )
+            for tap_no in range(KERNEL)
+        )
         grad_next = (
             grad_y.astype(jnp.float32) + back * elu_slope(stream_in.astype(jnp.float32))
         ).astype(jnp.bfloat16)

time: 322 us -> 318 us (0.988)
  matrix products: 14 us -> 22.4 us
  other arithmetic: 18.4 us -> 12 us
  local copies, waits for them, and re-layouts: 17.1 us -> 13.4 us
    dot_general x6 -> x42, matrix products: 5.14 us -> 13.5 us  [unit_back(): lax.dot_general(shifted_rows(gate, -(tap_no - half) * dilation, ids), wei...]
    transpose x4 -> x0, local copies, waits for them, and re-layouts: 6.97 us -> none  [unit_back(): jnp.transpose(weights_a[unit_idx], (0, 2, 1))]
    unnamed x48 -> x18, other arithmetic: 8.57 us -> 3.59 us
  transfers between devices with their start and end apart: 4 -> 4, of which waited for: 2 -> 3; matrix products, arithmetic and copies ran while one was open for 4% -> 3% of each run, Pallas kernels for 0% -> 0%
where the time goes in v8:
time: 318 us; the launch traced here: 316 us
  waiting for transfers between devices  246 us (77%)
  matrix products  22.4 us (7%)
  between operations  14.8 us (5%)
  local copies, waits for them, and re-layouts  13.4 us (4%)
  other arithmetic  12 us (4%)
  starting transfers between devices  7.17 us (2%)
    psum x1, waiting for transfers between devices, shards(): flat_a, flat_b = lax.psum((flat_a, flat_b), ('dp', 'seq'))  243 us
    dot_general x42, matrix products, unit_back(): lax.dot_general(shifted_rows(gate, -(tap_no - half) * dilation, ids), wei...  13.5 us
  transfers between devices with their start and end apart: 4, of which 3 were waited for; matrix products, arithmetic and copies ran while one was open for 3% of the time, Pallas kernels for 0%

profile of v8, /device:TPU:32, one launch (start us, length us, event | category | flops | bytes accessed | tf_op | source)
XLA Modules:
  0.0 316.1 jit_solution(1282582666395203757)
XLA Ops:
  7.2 0.9 pad_maximum_fusion.4
  8.2 3.8 %collective-permute-start = (bf16[120,512]{1,0:T(8,128)(2,1)S(1)}, bf16[120,512]{1,0:T(8,128)(2,1)S(1)}, u32[]{:S(2)}, u32[]{:S(2)}) collective-permute-start(bf16[120,512]{1,0:T(8,128)(2,1)S(1)} %get-tuple-element.9), channel_id=1, source_target_pairs={{0,2},{2,4},{4,6},{6,8},{8,10},{10,12},{12,14},{14,16},{16,18},{18... | collective-permute-start | bytes 368648 | tf_op jit(solution)/shard_map/ppermute | solution.py:18
  12.0 2.0 collective-permute-start.1
  14.0 0.7 copy.12
  15.2 2.9 fusion.300
  18.2 0.7 collective-permute-done.1
  20.7 1.0 fusion.29
  21.7 0.5 fusion.36
  23.7 1.0 fusion.30
  24.7 0.5 fusion.34
  26.7 0.9 broadcast_compare_fusion
  28.0 0.5 copy-done
  30.4 0.5 add_convert_fusion
  33.1 0.7 fusion.13
  36.1 0.5 fusion.33
  36.6 1.3 collective-permute-start.2
  38.0 2.1 collective-permute-done.2
  42.2 0.4 add_convert_fusion.2
  44.7 0.4 add_convert_fusion.1
  46.3 0.7 fusion.4
  47.0 0.7 fusion.2
  47.7 0.7 fusion
  48.4 0.4 convolution_bitcast_fusion
  48.9 1.0 pad_maximum_fusion
  49.8 2.8 maximum_bitcast_fusion
  52.7 1.0 slice_convert_fusion
  56.0 1.0 fusion.206
  56.9 243.4 %all-reduce.45.cloned.1.call-done = (f32[1,3,7,256,256]{4,3,2,1,0:T(8,128)}, f32[776,256]{1,0:T(8,128)}) async-done(((f32[1,3,7,256,256]{4,3,2,1,0:T(8,128)}, f32[776,256]{1,0:T(8,128)}), (f32[1,3,7,256,256]{4,3,2,1,0:T(8,128)}, f32[776,256]{1,0:T(8,128)})) %all-reduce.45.cloned.1.call-update) | async-done | bytes 6299664 | tf_op jit(solution)/shard_map/psum | solution.py:184
  300.3 2.1 slice.705
  302.4 0.7 slice.704
  303.1 0.6 broadcast_in_dim.451
  303.6 5.6 %copy.33 = f32[1,3,7,256,256]{4,3,2,1,0:T(8,128)} copy(f32[1,3,7,256,256]{4,3,2,1,0:T(8,128)} %get-tuple-element.55) | data formatting | bytes 11010048
  (106 shorter events, 19.3 us)
Async XLA Ops:
  7.2 293.1 %all-reduce.45.cloned.1.call-start = ((), (), s32[]{:S(2)}) async-start(), calls=%async_computation | async-start | bytes 12599296 | tf_op jit(solution)/shard_map/psum | solution.py:184
  8.2 10.0 %collective-permute-start = (bf16[120,512]{1,0:T(8,128)(2,1)S(1)}, bf16[120,512]{1,0:T(8,128)(2,1)S(1)}, u32[]{:S(2)}, u32[]{:S(2)}) collective-permute-start(bf16[120,512]{1,0:T(8,128)(2,1)S(1)} %get-tuple-element.9), channel_id=1, source_target_pairs={{0,2},{2,4},{4,6},{6,8},{8,10},{10,12},{12,14},{14,16},{16,18},{18... | collective-permute-start | bytes 368648 | tf_op jit(solution)/shard_map/ppermute | solution.py:18
  12.0 6.9 %collective-permute-start.1 = (bf16[120,512]{1,0:T(8,128)(2,1)S(1)}, bf16[120,512]{1,0:T(8,128)(2,1)S(1)}, u32[]{:S(2)}, u32[]{:S(2)}) collective-permute-start(bf16[120,512]{1,0:T(8,128)(2,1)S(1)} %get-tuple-element.10), channel_id=1, source_target_pairs={{2,0},{4,2},{6,4},{8,6},{10,8},{12,10},{14,12},{16,14},{18,16},{20... | collective-permute-start | bytes 368648 | tf_op jit(solution)/shard_map/ppermute | solution.py:20
  15.2 2.9 copy-start.9
  15.2 3.6 %copy-start.2 = (bf16[1,1,512,256]{3,2,1,0:T(8,128)(2,1)S(1)}, bf16[1,1,512,256]{3,2,1,0:T(8,128)(2,1)}, u32[]{:S(2)}) copy-start(bf16[1,1,512,256]{3,2,1,0:T(8,128)(2,1)} %param.6) | copy-start | bytes 786436
  15.2 3.6 %copy-start.3 = (bf16[1,512,256]{2,1,0:T(8,128)(2,1)S(1)}, bf16[1,512,256]{2,1,0:T(8,128)(2,1)}, u32[]{:S(2)}) copy-start(bf16[1,512,256]{2,1,0:T(8,128)(2,1)} %param.7) | copy-start | bytes 786436
  18.9 17.2 %copy-start.1 = (bf16[752,512]{1,0:T(8,128)(2,1)}, bf16[752,512]{1,0:T(8,128)(2,1)S(1)}, u32[]{:S(2)}) copy-start(bf16[752,512]{1,0:T(8,128)(2,1)S(1)} %pad_maximum_fusion.2) | copy-start | bytes 2310148
  20.7 1.0 copy-start.10
  25.2 1.4 copy-start.4
  26.7 1.8 copy-start
  36.5 1.5 copy-start.7
  36.6 3.6 %collective-permute-start.2 = (bf16[752,256]{1,0:T(8,128)(2,1)S(1)}, bf16[752,256]{1,0:T(8,128)(2,1)S(1)}, u32[]{:S(2)}, u32[]{:S(2)}) collective-permute-start(bf16[752,256]{1,0:T(8,128)(2,1)S(1)} %fusion.33), channel_id=1, source_target_pairs={{1,0},{3,2},{5,4},{7,6},{9,8},{11,10},{13,12},{15,14},{17,16},{19,... | collective-permute-start | bytes 1155080 | tf_op jit(solution)/shard_map/ppermute | solution.py:149
  45.1 1.1 copy-start.5
  54.9 1.0 copy-start.6
  54.9 1.1 copy-start.8
Sparse Core Ops, SparseCore 0:
  52.8 247.4 all-reduce.44

commit v9 on v8

--- a/solution.py
+++ b/solution.py
@@ -94,14 +94,12 @@
     for unit_idx in range(UNITS):
         dilation = 3**unit_idx
         active = elu_act(stream.astype(jnp.float32)).astype(jnp.bfloat16)
-        tap_rows = jnp.concatenate(
-            [shifted_rows(active, (tap_no - half) * dilation) for tap_no in range(KERNEL)],
-            axis=1,
-        )
-        pre_act = biases_a[unit_idx][None, :] + jnp.dot(
-            tap_rows,
-            weights_a[unit_idx].reshape(KERNEL * channels, inner),
-            preferred_element_type=jnp.float32,
+        tap_rows = [
+            shifted_rows(active, (tap_no - half) * dilation) for tap_no in range(KERNEL)
+        ]
+        pre_act = biases_a[unit_idx][None, :] + sum(
+            jnp.dot(tap_rows[tap_no], weights_a[unit_idx, tap_no], preferred_element_type=jnp.float32)
+            for tap_no in range(KERNEL)
         )
         squashed = elu_act(pre_act).astype(jnp.bfloat16)
         next_stream = (
@@ -163,9 +161,12 @@
             squashed[own], grad_out, contract, preferred_element_type=jnp.float32
         )
         unit_bias = jnp.sum(gate.astype(jnp.float32), axis=0)
-        unit_a = lax.dot_general(
-            tap_rows[own], gate, contract, preferred_element_type=jnp.float32
-        ).reshape(KERNEL, channels, inner)
+        unit_a = jnp.stack(
+            [
+                lax.dot_general(rows[own], gate, contract, preferred_element_type=jnp.float32)
+                for rows in tap_rows
+            ]
+        )
         grads_a[unit_idx] = unit_a
         grads_bias[unit_idx] = unit_bias
         grads_b[unit_idx] = unit_b

time: 318 us -> 325 us (1.022)
  matrix products: 22.4 us -> 29.6 us
    dot_general x6 -> x42, matrix products: 5.01 us -> 12.3 us  [the longest x21 6.65 us: shards(): jnp.dot(tap_rows[tap_no], weights_a[unit_idx, tap_no], preferred_element_...]
    unnamed x18 -> x0, other arithmetic: 3.59 us -> none
    select_n x0 -> x3, other arithmetic: none -> 3.45 us  [shifted_rows(): jnp.where(linked(shift_by, ids), padded[edge + shift_by:edge + shift_by +...]
  transfers between devices with their start and end apart: 4 -> 4, of which waited for: 3 -> 3; matrix products, arithmetic and copies ran while one was open for 3% -> 2% of each run, Pallas kernels for 0% -> 0%
where the time goes in v9:
time: 325 us; the launch traced here: 323 us
  waiting for transfers between devices  248 us (76%)
  matrix products  29.6 us (9%)
  between operations  14.9 us (5%)
  other arithmetic  12.4 us (4%)
  local copies, waits for them, and re-layouts  10.7 us (3%)
  starting transfers between devices  7.66 us (2%)
    psum x1, waiting for transfers between devices, shards(): flat_a, flat_b = lax.psum((flat_a, flat_b), ('dp', 'seq'))  243 us
    dot_general x42, matrix products, unit_back(): lax.dot_general(shifted_rows(gate, -(tap_no - half) * dilation, ids), wei...  13.4 us
    dot_general x21, matrix products, shards(): jnp.dot(tap_rows[tap_no], weights_a[unit_idx, tap_no], preferred_element_...  6.65 us
  transfers between devices with their start and end apart: 4, of which 3 were waited for; matrix products, arithmetic and copies ran while one was open for 2% of the time, Pallas kernels for 0%

profile of v9, /device:TPU:32, one launch (start us, length us, event | category | flops | bytes accessed | tf_op | source)
XLA Modules:
  0.0 322.9 jit_solution(7751271832326582518)
XLA Ops:
  7.2 0.9 pad_maximum_fusion.4
  8.2 4.1 %collective-permute-start = (bf16[120,512]{1,0:T(8,128)(2,1)S(1)}, bf16[120,512]{1,0:T(8,128)(2,1)S(1)}, u32[]{:S(2)}, u32[]{:S(2)}) collective-permute-start(bf16[120,512]{1,0:T(8,128)(2,1)S(1)} %get-tuple-element.12), channel_id=1, source_target_pairs={{0,2},{2,4},{4,6},{6,8},{8,10},{10,12},{12,14},{14,16},{16,18},{18... | collective-permute-start | bytes 368648 | tf_op jit(solution)/shard_map/ppermute | solution.py:18
  12.3 2.0 collective-permute-start.1
  14.3 0.7 copy.12
  15.5 0.7 fusion.345
  16.2 2.9 collective-permute-done.1
  19.1 1.1 pad_maximum_fusion.2
  20.5 1.0 slice_select_fusion.13
  22.4 0.5 convolution_add_fusion.33
  23.4 0.5 fusion.47
  24.1 0.5 fusion.54
  24.6 1.1 slice_select_fusion.7
  26.5 0.5 convolution_add_fusion.27
  27.5 0.5 fusion.48
  28.0 0.5 fusion.52
  28.6 1.4 slice_select_fusion.1
  30.7 0.5 convolution_add_fusion.21
  34.4 0.5 add_convert_fusion
  37.1 0.5 fusion.10
  39.9 0.5 fusion.51
  40.4 1.5 collective-permute-start.2
  42.0 1.9 collective-permute-done.2
  56.0 0.4 convolution_bitcast_fusion
  56.5 1.0 pad_maximum_fusion
  57.4 2.8 maximum_bitcast_fusion
  60.3 1.0 slice_convert_fusion
  63.4 1.0 fusion.245
  64.3 242.8 %all-reduce.45.cloned.1.call-done = (f32[1,3,7,256,256]{4,3,2,1,0:T(8,128)}, f32[776,256]{1,0:T(8,128)}) async-done(((f32[1,3,7,256,256]{4,3,2,1,0:T(8,128)}, f32[776,256]{1,0:T(8,128)}), (f32[1,3,7,256,256]{4,3,2,1,0:T(8,128)}, f32[776,256]{1,0:T(8,128)})) %all-reduce.45.cloned.1.call-update) | async-done | bytes 6299664 | tf_op jit(solution)/shard_map/psum | solution.py:185
  307.1 2.1 slice.801
  309.2 0.7 slice.800
  309.9 0.6 broadcast_in_dim.451
  310.4 5.6 %copy.33 = f32[1,3,7,256,256]{4,3,2,1,0:T(8,128)} copy(f32[1,3,7,256,256]{4,3,2,1,0:T(8,128)} %get-tuple-element.76) | data formatting | bytes 11010048
  (113 shorter events, 25.9 us)
Async XLA Ops:
  7.2 299.9 %all-reduce.45.cloned.1.call-start = ((), (), s32[]{:S(2)}) async-start(), calls=%async_computation | async-start | bytes 12599296 | tf_op jit(solution)/shard_map/psum | solution.py:185
  8.2 13.4 %copy-start = (bf16[1,3,7,256,256]{4,3,2,1,0:T(8,128)(2,1)S(1)}, bf16[1,3,7,256,256]{4,3,2,1,0:T(8,128)(2,1)}, u32[]{:S(2)}) copy-start(bf16[1,3,7,256,256]{4,3,2,1,0:T(8,128)(2,1)} %param.9) | copy-start | bytes 8257540
  8.2 8.1 %collective-permute-start = (bf16[120,512]{1,0:T(8,128)(2,1)S(1)}, bf16[120,512]{1,0:T(8,128)(2,1)S(1)}, u32[]{:S(2)}, u32[]{:S(2)}) collective-permute-start(bf16[120,512]{1,0:T(8,128)(2,1)S(1)} %get-tuple-element.12), channel_id=1, source_target_pairs={{0,2},{2,4},{4,6},{6,8},{8,10},{10,12},{12,14},{14,16},{16,18},{18... | collective-permute-start | bytes 368648 | tf_op jit(solution)/shard_map/ppermute | solution.py:18
  12.3 6.9 %collective-permute-start.1 = (bf16[120,512]{1,0:T(8,128)(2,1)S(1)}, bf16[120,512]{1,0:T(8,128)(2,1)S(1)}, u32[]{:S(2)}, u32[]{:S(2)}) collective-permute-start(bf16[120,512]{1,0:T(8,128)(2,1)S(1)} %get-tuple-element.13), channel_id=1, source_target_pairs={{2,0},{4,2},{6,4},{8,6},{10,8},{12,10},{14,12},{16,14},{18,16},{20... | collective-permute-start | bytes 368648 | tf_op jit(solution)/shard_map/ppermute | solution.py:20
  20.2 19.7 %copy-start.1 = (bf16[752,512]{1,0:T(8,128)(2,1)}, bf16[752,512]{1,0:T(8,128)(2,1)S(1)}, u32[]{:S(2)}) copy-start(bf16[752,512]{1,0:T(8,128)(2,1)S(1)} %pad_maximum_fusion.2) | copy-start | bytes 2310148
  23.1 1.0 copy-start.5
  40.4 4.5 %copy-start.3 = (bf16[752,256]{1,0:T(8,128)(2,1)}, bf16[752,256]{1,0:T(8,128)(2,1)S(1)}, u32[]{:S(2)}) copy-start(bf16[752,256]{1,0:T(8,128)(2,1)S(1)} %fusion.51) | copy-start | bytes 1155076
  40.4 3.6 %collective-permute-start.2 = (bf16[752,256]{1,0:T(8,128)(2,1)S(1)}, bf16[752,256]{1,0:T(8,128)(2,1)S(1)}, u32[]{:S(2)}, u32[]{:S(2)}) collective-permute-start(bf16[752,256]{1,0:T(8,128)(2,1)S(1)} %fusion.51), channel_id=1, source_target_pairs={{1,0},{3,2},{5,4},{7,6},{9,8},{11,10},{13,12},{15,14},{17,16},{19,... | collective-permute-start | bytes 1155080 | tf_op jit(solution)/shard_map/ppermute | solution.py:147
  54.0 2.0 copy-start.2
  62.2 1.2 copy-start.4
Sparse Core Ops, SparseCore 0:
  60.4 246.6 all-reduce.44
